TPU v7x, 256 devices: a whole 4x4x8 slice. The times are simulated.
256 devices in a mesh: dp: 4 (over y), tp: 64 (over x, z, core).
Axes of the slice: x: 4, y: 4, z: 8, core: 2. Of those that a mesh axis runs over, the one named last changes fastest.
Arguments:
- attn_heads: bfloat16 [4, 8192, 2048], P(None, 'tp', 'dp'), may hold values from -1.5 to 1.5
- w_out: bfloat16 [2048, 2048], P('dp'), may hold values from -0.125 to 0.125
- residual: bfloat16 [32768, 2048], P(('dp', 'tp')), may hold values from -1.5 to 1.5
- moe_gain: float32 [2048], replicated, may hold values from 0.1 to 1.9
- router: bfloat16 [2048, 64], replicated, may hold values from -0.0625 to 0.0625
- expert_ids: int32 [32768, 8], P(('dp', 'tp')), may hold values from 0 to 63, all different within a row; in each aligned block of 128 rows (0 to 127, 128 to 255, ...) at most 24 rows name the same one
- w_gate_up: bfloat16 [64, 2048, 1024], P('tp'), may hold values from -0.125 to 0.125
- w_down: bfloat16 [64, 512, 2048], P('tp'), may hold values from -0.75 to 0.75
- next_gain: float32 [2048], replicated, may hold values from 0.1 to 1.9
Outputs:
- layer_out: bfloat16 [32768, 2048], P(('dp', 'tp'))
- next_input: bfloat16 [4, 8192, 2048], P(None, 'tp')
Inputs may be any that keep to these rules, and one draw needn't show every extreme that they name: `expert_ids`: each row names 8 different experts. In each aligned block of 128 rows (the rows of one device) no expert is named by more than 24 rows, a bound that some block reaches.
All inputs are finite; a program needn't handle non-finite values.
Results may differ from a plain program's by a relative error of at most 0.0095.
Values may be sent and summed in bfloat16 or wider, within the bound.
No kernel may reach another device: no remote copies, remote signals or barrier semaphores. Data moves between devices by JAX's collectives and lax.ppermute only.
A program may use at most 128 MiB of HBM per device.

v0:
```python
import jax
import jax.numpy as jnp
from jax import lax
from jax.sharding import PartitionSpec as P


EPS = 1e-05


def rms_scale(values, gain_vector):
    mean_square = jnp.mean(values * values, axis=-1, keepdims=True)
    return values * lax.rsqrt(mean_square + EPS) * gain_vector


def split_hi_lo(values):
    high = values.astype(jnp.bfloat16)
    low = (values - high.astype(jnp.float32)).astype(jnp.bfloat16)
    return high, low


def dp_reduce(heads, weights):
    ring = heads.shape[0]
    here = lax.axis_index("dp")

    def product(group):
        rows = lax.dynamic_index_in_dim(heads, group, axis=0, keepdims=False)
        return jnp.dot(rows, weights, preferred_element_type=jnp.float32)

    total = product(here)
    for shift in range(1, ring):
        pairs = [(j, (j + shift) % ring) for j in range(ring)]
        total = total + lax.ppermute(product((here + shift) % ring), "dp", pairs)
    return total


def dp_gather(block):
    ring = lax.axis_size("dp")
    here = lax.axis_index("dp")
    received = [block]
    for shift in range(1, ring):
        pairs = [(j, (j + shift) % ring) for j in range(ring)]
        received.append(lax.ppermute(block, "dp", pairs))
    order = (here - jnp.arange(ring, dtype=jnp.int32)) % ring
    return jnp.take(jnp.stack(received), order, axis=0)


def local(attn_heads, w_out, residual, moe_gain, router, expert_ids, w_gate_up, w_down, next_gain):
    groups, tok_rows, quarter = attn_heads.shape
    feat_width = w_out.shape[1]
    experts = router.shape[1]
    top_count = expert_ids.shape[1]
    capacity = min(tok_rows, 3 * tok_rows * top_count // (2 * experts))
    slots = experts * capacity

    expert_pos = jnp.arange(experts, dtype=jnp.int32)
    chosen = expert_ids[:, :, None] == expert_pos[None, None, :]
    member = jnp.sum(chosen.astype(jnp.float32), axis=1)
    row_pos = jnp.arange(tok_rows, dtype=jnp.int32)
    earlier = (row_pos[None, :] < row_pos[:, None]).astype(jnp.bfloat16)
    row_ranks = jnp.dot(
        earlier, member.astype(jnp.bfloat16), preferred_element_type=jnp.float32
    ).astype(jnp.int32)
    slot_pos = jnp.arange(capacity, dtype=jnp.int32)
    placed = (member.T[:, None, :] > 0) & (row_ranks.T[:, None, :] == slot_pos[None, :, None])
    dispatch = placed.reshape(slots, tok_rows).astype(jnp.bfloat16)

    first = feat_width // 4
    bounds = [(0, first), (first, feat_width)]
    flat_heads = attn_heads.reshape(groups * tok_rows, quarter)
    partial = jnp.dot(flat_heads, w_out[:, :first], preferred_element_type=jnp.float32)
    pieces = lax.all_to_all(
        partial.reshape(groups, tok_rows, first), "dp", split_axis=0, concat_axis=0, tiled=True
    )
    part = jnp.sum(pieces, axis=0)
    mid_parts = []
    arrived_parts = []
    for c, (lo, hi) in enumerate(bounds):
        res_c, part = lax.optimization_barrier((residual[:, lo:hi], part))
        mid_c = (res_c.astype(jnp.float32) + part).astype(jnp.bfloat16)
        mid_parts.append(mid_c)
        outgoing = jnp.dot(dispatch, mid_c, preferred_element_type=jnp.float32).astype(jnp.bfloat16)
        if c == 0:
            outgoing, heads_now = lax.optimization_barrier((outgoing, attn_heads))
            part = dp_reduce(heads_now, w_out[:, first:])
        arrived_parts.append(
            lax.all_to_all(
                outgoing.reshape(experts, capacity, hi - lo), "tp", split_axis=0, concat_axis=0, tiled=True
            ).reshape(slots, hi - lo)
        )
    mid_wide = jnp.concatenate(mid_parts, axis=1).astype(jnp.float32)
    normed = rms_scale(mid_wide, moe_gain).astype(jnp.bfloat16)
    logits = jnp.dot(normed, router, preferred_element_type=jnp.float32)

    picked = jnp.sum(jnp.where(chosen, logits[:, None, :], 0.0), axis=2)
    raised = jnp.exp(picked)
    gate_weights = raised / jnp.sum(raised, axis=1, keepdims=True)
    weight_full = jnp.sum(jnp.where(chosen, gate_weights[:, :, None], 0.0), axis=1)
    combine = jnp.where(placed, weight_full.T[:, None, :], 0.0).reshape(slots, tok_rows)
    combine_hi, combine_lo = split_hi_lo(combine)

    arrived_mid = jnp.concatenate(arrived_parts, axis=1).astype(jnp.float32)
    arrived = rms_scale(arrived_mid, moe_gain).astype(jnp.bfloat16)

    gate_up = w_gate_up[0]
    down_proj = w_down[0]
    hidden_width = down_proj.shape[0]
    projected_up = jnp.dot(arrived, gate_up, preferred_element_type=jnp.float32)
    activated = (
        jax.nn.silu(projected_up[:, :hidden_width]) * projected_up[:, hidden_width:]
    ).astype(jnp.bfloat16)
    served = jnp.dot(activated, down_proj, preferred_element_type=jnp.float32).astype(jnp.bfloat16)

    served, combine_hi, combine_lo = lax.optimization_barrier((served, combine_hi, combine_lo))
    returned = lax.all_to_all(
        served.reshape(experts, capacity, feat_width), "tp", split_axis=0, concat_axis=0, tiled=True
    ).reshape(slots, feat_width)
    dims = (((0,), (0,)), ((), ()))
    expert_sum = lax.dot_general(
        combine_hi, returned, dims, preferred_element_type=jnp.float32
    ) + lax.dot_general(combine_lo, returned, dims, preferred_element_type=jnp.float32)

    layer_sum = mid_wide + expert_sum
    layer_out = layer_sum.astype(jnp.bfloat16)
    next_local = rms_scale(layer_sum, next_gain).astype(jnp.bfloat16)
    next_input = dp_gather(next_local)
    return (layer_out, next_input)


def solution(mesh):
    in_specs = (
        P(None, "tp", "dp"),
        P("dp", None),
        P(("dp", "tp"), None),
        P(),
        P(),
        P(("dp", "tp"), None),
        P("tp", None, None),
        P("tp", None, None),
        P(),
    )
    out_specs = (P(("dp", "tp"), None), P(None, "tp", None))

    return jax.shard_map(local, mesh=mesh, in_specs=in_specs, out_specs=out_specs, check_vma=False)
```

profile of v0, /device:TPU:1, one launch (start us, length us, event | category | flops | bytes accessed | tf_op | source)
XLA Modules:
  0.0 410.5 jit_solution(673122350042327967)
XLA Ops:
  0.6 0.0 copy-start
  0.6 0.0 slice-start
  0.7 2.8 fusion.31
  3.4 5.0 %all-to-all-start = ((f32[4,128,512]{2,1,0:T(8,128)}), f32[4,128,512]{2,1,0:T(8,128)S(1)}, u32[]{:S(2)}, u32[]{:S(2)}) async-start(f32[4,128,512]{2,1,0:T(8,128)} %fusion.31), calls=%async_computation | async-start | bytes 2097152 | tf_op jit(solution)/shard_map/all_to_all | solution.py:71
  8.4 0.1 eq.46
  8.6 0.1 convolution_convert_fusion.3
  8.7 1.0 fusion.28
  9.7 12.2 %all-to-all-done = f32[4,128,512]{2,1,0:T(8,128)S(1)} async-done(((f32[4,128,512]{2,1,0:T(8,128)}), f32[4,128,512]{2,1,0:T(8,128)S(1)}, u32[]{:S(2)}, u32[]{:S(2)}) %all-to-all-start) | async-done | bytes 1048608 | tf_op jit(solution)/shard_map/all_to_all | solution.py:71
  21.9 0.8 reduce_sum.72
  22.7 1.0 add_convert_fusion.1
  23.8 2.6 convolution_convert_fusion.2
  26.4 14.2 %all-to-all-start.1 = ((bf16[64,24,512]{2,1,0:T(8,128)(2,1)}), bf16[64,24,512]{2,1,0:T(8,128)(2,1)}, u32[]{:S(2)}, u32[]{:S(2)}) async-start(bf16[64,24,512]{2,1,0:T(8,128)(2,1)} %bitcast.74), calls=%async_computation.1 | async-start | bytes 3145728 | tf_op jit(solution)/shard_map/all_to_all | solution.py:86
  40.6 0.0 copy-start.1
  40.7 2.8 fusion.22
  43.5 0.3 collective-permute-start
  43.8 2.7 fusion.20
  46.4 1.8 collective-permute-start.1
  48.2 1.3 fusion.18
  49.5 0.6 collective-permute-start.2
  50.1 14.1 %collective-permute-done = f32[128,1536]{1,0:T(8,128)} collective-permute-done((f32[128,1536]{1,0:T(8,128)}, f32[128,1536]{1,0:T(8,128)}, u32[]{:S(2)}, u32[]{:S(2)}) %collective-permute-start) | collective-permute-done | bytes 786464 | tf_op jit(solution)/shard_map/ppermute | solution.py:32
  64.2 15.7 %collective-permute-done.1 = f32[128,1536]{1,0:T(8,128)} collective-permute-done((f32[128,1536]{1,0:T(8,128)}, f32[128,1536]{1,0:T(8,128)}, u32[]{:S(2)}, u32[]{:S(2)}) %collective-permute-start.1) | collective-permute-done | bytes 786464 | tf_op jit(solution)/shard_map/ppermute | solution.py:32
  79.9 3.7 collective-permute-done.2
  83.6 2.5 fusion.10
  86.1 0.1 add_convert_fusion
  86.2 3.5 convolution_convert_fusion.1
  89.7 0.0 all-to-all-done.1
  89.7 11.8 %all-to-all-start.2 = ((bf16[64,24,1536]{2,1,0:T(8,128)(2,1)}), bf16[64,24,1536]{2,1,0:T(8,128)(2,1)}, u32[]{:S(2)}, u32[]{:S(2)}) async-start(bf16[64,24,1536]{2,1,0:T(8,128)(2,1)} %bitcast.72), calls=%async_computation.2 | async-start | bytes 9437184 | tf_op jit(solution)/shard_map/all_to_all | solution.py:86
  101.5 0.2 fusion.15
  101.7 0.4 fusion.29
  102.2 0.3 fusion.27
  102.5 0.3 fusion.26
  102.8 105.8 %all-to-all-done.2 = bf16[64,24,1536]{2,1,0:T(8,128)(2,1)} async-done(((bf16[64,24,1536]{2,1,0:T(8,128)(2,1)}), bf16[64,24,1536]{2,1,0:T(8,128)(2,1)}, u32[]{:S(2)}, u32[]{:S(2)}) %all-to-all-start.2) | async-done | bytes 4718624 | tf_op jit(solution)/shard_map/all_to_all | solution.py:86
  208.6 4.4 %fusion = f32[1536]{0:T(1024)S(1)} fusion(bf16[1536,1536]{1,0:T(8,128)(2,1)} %bitcast.11, bf16[1536,512]{1,0:T(8,128)(2,1)} %bitcast.9), kind=kLoop, calls=%fused_computation.3 | loop fusion | flops 18872832 | bytes 6297600 | tf_op jit(solution)/shard_map/reduce_sum | solution.py:11
  213.0 9.0 %fusion.3 = f32[1536,1024]{1,0:T(8,128)S(1)} fusion(f32[2048]{0:T(1024)S(1)} %copy-done.8, f32[1536]{0:T(1024)S(1)} %add_rsqrt_fusion, bf16[1,2048,1024]{2,1,0:T(8,128)(2,1)S(1)} %copy-done.6, bf16[1536,1536]{1,0:T(8,128)(2,1)} %bitcast.11, bf16[1536,512]{1,0:T(8,128)(2,1)} %bitcast.9), kind=kOutput, calls=%fused_computation.8 | convolution fusion | flops 6464471040 | bytes 16791552 | tf_op jit(solution)/shard_map/dot_general | solution.py:107
  222.1 3.7 convolution_convert_fusion
  225.8 146.7 %all_to_all.20 = bf16[64,24,2048]{2,1,0:T(8,128)(2,1)S(1)} all-to-all(bf16[64,24,2048]{2,1,0:T(8,128)(2,1)S(1)} %bitcast.73), channel_id=1, replica_groups=mesh['dp'=4,'tp'=64] {'tp'}, dimensions={0} | all-to-all | bytes 12582912 | tf_op jit(solution)/shard_map/all_to_all | solution.py:114
  372.5 1.0 fusion.55
  373.5 0.0 copy-start.5
  373.5 1.1 multiply_reduce_fusion
  374.7 1.0 multiply_convert_fusion
  375.7 0.0 collective-permute-start.3
  375.7 3.5 collective-permute-start.4
  379.2 0.0 collective-permute-start.5
  379.3 10.7 %collective-permute-done.3 = bf16[128,2048]{1,0:T(8,128)(2,1)S(1)} collective-permute-done((bf16[128,2048]{1,0:T(8,128)(2,1)S(1)}, bf16[128,2048]{1,0:T(8,128)(2,1)S(1)}, u32[]{:S(2)}, u32[]{:S(2)}) %collective-permute-start.3) | collective-permute-done | bytes 524320 | tf_op jit(solution)/shard_map/ppermute | solution.py:42
  390.0 12.1 %collective-permute-done.4 = bf16[128,2048]{1,0:T(8,128)(2,1)S(1)} collective-permute-done((bf16[128,2048]{1,0:T(8,128)(2,1)S(1)}, bf16[128,2048]{1,0:T(8,128)(2,1)S(1)}, u32[]{:S(2)}, u32[]{:S(2)}) %collective-permute-start.4) | collective-permute-done | bytes 524320 | tf_op jit(solution)/shard_map/ppermute | solution.py:42
  402.1 1.6 pad_maximum_fusion.2
  403.7 3.6 gather_fusion
  407.3 3.2 broadcast_select_fusion
  (32 shorter events, 0.2 us)
Async XLA Ops:
  0.6 221.4 %copy-start = (bf16[1,512,2048]{2,1,0:T(8,128)(2,1)S(1)}, bf16[1,512,2048]{2,1,0:T(8,128)(2,1)}, u32[]{:S(2)}) copy-start(bf16[1,512,2048]{2,1,0:T(8,128)(2,1)} %param.16) | copy-start | bytes 6291460
  0.6 22.1 %slice-start = ((bf16[128,2048]{1,0:T(8,128)(2,1)}), bf16[128,512]{1,0:T(8,128)(2,1)S(1)}, s32[]{:S(2)}) async-start(bf16[128,2048]{1,0:T(8,128)(2,1)} %param.11), calls=%async_computation.4 | async-start | bytes 262144 | tf_op jit(solution)/shard_map/slice | solution.py:78
  0.7 7.9 %copy-start.4 = (s32[128,8]{0,1:T(8,128)S(1)}, s32[128,8]{0,1:T(8,128)}, u32[]{:S(2)}) copy-start(s32[128,8]{0,1:T(8,128)} %param.14) | copy-start | bytes 12292
  3.4 18.5 %all-to-all-start = ((f32[4,128,512]{2,1,0:T(8,128)}), f32[4,128,512]{2,1,0:T(8,128)S(1)}, u32[]{:S(2)}, u32[]{:S(2)}) async-start(f32[4,128,512]{2,1,0:T(8,128)} %fusion.31), calls=%async_computation | async-start | bytes 2097152 | tf_op jit(solution)/shard_map/all_to_all | solution.py:71
  22.7 17.9 %copy-start.2 = (bf16[4,128,512]{2,1,0:T(8,128)(2,1)S(1)}, bf16[4,128,512]{2,1,0:T(8,128)(2,1)}, u32[]{:S(2)}) copy-start(bf16[4,128,512]{2,1,0:T(8,128)(2,1)} %param.9) | copy-start | bytes 1572868
  26.4 63.3 %all-to-all-start.1 = ((bf16[64,24,512]{2,1,0:T(8,128)(2,1)}), bf16[64,24,512]{2,1,0:T(8,128)(2,1)}, u32[]{:S(2)}, u32[]{:S(2)}) async-start(bf16[64,24,512]{2,1,0:T(8,128)(2,1)} %bitcast.74), calls=%async_computation.1 | async-start | bytes 3145728 | tf_op jit(solution)/shard_map/all_to_all | solution.py:86
  40.6 7.6 %copy-start.1 = (bf16[512,2048]{1,0:T(8,128)(2,1)S(1)}, bf16[512,2048]{1,0:T(8,128)(2,1)}, u32[]{:S(2)}) copy-start(bf16[512,2048]{1,0:T(8,128)(2,1)} %param.10) | copy-start | bytes 6291460
  43.5 20.7 %collective-permute-start = (f32[128,1536]{1,0:T(8,128)}, f32[128,1536]{1,0:T(8,128)}, u32[]{:S(2)}, u32[]{:S(2)}) collective-permute-start(f32[128,1536]{1,0:T(8,128)} %fusion.22), channel_id=1, source_target_pairs={{0,64},{64,128},{128,192},{192,0},{1,65},{65,129},{129,193},{193,1... | collective-permute-start | bytes 2359304 | tf_op jit(solution)/shard_map/ppermute | solution.py:32
  46.4 33.5 %collective-permute-start.1 = (f32[128,1536]{1,0:T(8,128)}, f32[128,1536]{1,0:T(8,128)}, u32[]{:S(2)}, u32[]{:S(2)}) collective-permute-start(f32[128,1536]{1,0:T(8,128)} %fusion.20), channel_id=1, source_target_pairs={{0,128},{64,192},{128,0},{192,64},{1,129},{65,193},{129,1},{193,65... | collective-permute-start | bytes 2359304 | tf_op jit(solution)/shard_map/ppermute | solution.py:32
  49.5 36.6 %slice-start.1 = ((bf16[128,2048]{1,0:T(8,128)(2,1)}), bf16[128,1536]{1,0:T(8,128)(2,1)S(1)}, s32[]{:S(2)}) async-start(bf16[128,2048]{1,0:T(8,128)(2,1)} %param.11), calls=%async_computation.5 | async-start | bytes 786432 | tf_op jit(solution)/shard_map/slice | solution.py:78
  49.5 34.1 %collective-permute-start.2 = (f32[128,1536]{1,0:T(8,128)}, f32[128,1536]{1,0:T(8,128)}, u32[]{:S(2)}, u32[]{:S(2)}) collective-permute-start(f32[128,1536]{1,0:T(8,128)} %fusion.18), channel_id=1, source_target_pairs={{0,192},{64,0},{128,64},{192,128},{1,193},{65,1},{129,65},{193,129... | collective-permute-start | bytes 2359304 | tf_op jit(solution)/shard_map/ppermute | solution.py:32
  50.1 36.1 %copy-start.3 = (pred[1536,128]{1,0:T(32,128)(4,1)S(1)}, pred[1536,128]{1,0:T(32,128)(4,1)}, u32[]{:S(2)}) copy-start(pred[1536,128]{1,0:T(32,128)(4,1)} %fusion.28) | copy-start | bytes 589828
  89.7 12.0 %copy-start.7 = (bf16[2048,64]{0,1:T(8,128)(2,1)S(1)}, bf16[2048,64]{0,1:T(8,128)(2,1)}, u32[]{:S(2)}) copy-start(bf16[2048,64]{0,1:T(8,128)(2,1)} %param.13) | copy-start | bytes 786436
  89.7 12.0 %copy-start.8 = (f32[2048]{0:T(1024)S(1)}, f32[2048]{0:T(1024)}, u32[]{:S(2)}) copy-start(f32[2048]{0:T(1024)} %param.12) | copy-start | bytes 24580
  89.7 118.9 %all-to-all-start.2 = ((bf16[64,24,1536]{2,1,0:T(8,128)(2,1)}), bf16[64,24,1536]{2,1,0:T(8,128)(2,1)}, u32[]{:S(2)}, u32[]{:S(2)}) async-start(bf16[64,24,1536]{2,1,0:T(8,128)(2,1)} %bitcast.72), calls=%async_computation.2 | async-start | bytes 9437184 | tf_op jit(solution)/shard_map/all_to_all | solution.py:86
  208.6 4.4 %copy-start.6 = (bf16[1,2048,1024]{2,1,0:T(8,128)(2,1)S(1)}, bf16[1,2048,1024]{2,1,0:T(8,128)(2,1)}, u32[]{:S(2)}) copy-start(bf16[1,2048,1024]{2,1,0:T(8,128)(2,1)} %param.15) | copy-start | bytes 12582916
  373.5 1.2 copy-start.5
  375.7 14.3 %collective-permute-start.3 = (bf16[128,2048]{1,0:T(8,128)(2,1)S(1)}, bf16[128,2048]{1,0:T(8,128)(2,1)S(1)}, u32[]{:S(2)}, u32[]{:S(2)}) collective-permute-start(bf16[128,2048]{1,0:T(8,128)(2,1)S(1)} %get-tuple-element.20), channel_id=1, source_target_pairs={{0,64},{64,128},{128,192},{192,0},{1,65},{65,129},{129,193},{193,1... | collective-permute-start | bytes 1572872 | tf_op jit(solution)/shard_map/ppermute | solution.py:42
  375.7 26.4 %collective-permute-start.4 = (bf16[128,2048]{1,0:T(8,128)(2,1)S(1)}, bf16[128,2048]{1,0:T(8,128)(2,1)S(1)}, u32[]{:S(2)}, u32[]{:S(2)}) collective-permute-start(bf16[128,2048]{1,0:T(8,128)(2,1)S(1)} %get-tuple-element.20), channel_id=1, source_target_pairs={{0,128},{64,192},{128,0},{192,64},{1,129},{65,193},{129,1},{193,65... | collective-permute-start | bytes 1572872 | tf_op jit(solution)/shard_map/ppermute | solution.py:42
  379.2 22.9 %collective-permute-start.5 = (bf16[128,2048]{1,0:T(8,128)(2,1)S(1)}, bf16[128,2048]{1,0:T(8,128)(2,1)S(1)}, u32[]{:S(2)}, u32[]{:S(2)}) collective-permute-start(bf16[128,2048]{1,0:T(8,128)(2,1)S(1)} %get-tuple-element.20), channel_id=1, source_target_pairs={{0,192},{64,0},{128,64},{192,128},{1,193},{65,1},{129,65},{193,129... | collective-permute-start | bytes 1572872 | tf_op jit(solution)/shard_map/ppermute | solution.py:42
where the time goes:
time: 411 us; the launch traced here: 410 us
  waiting for transfers between devices  174 us (42%)
  blocking collectives  147 us (36%)
  starting transfers between devices  37.2 us (9%)
  matrix products  33.5 us (8%)
  other arithmetic  14 us (3%)
    all_to_all x1, blocking collectives, local(): lax.all_to_all(served.reshape(experts, capacity, feat_width), 'tp', split...  147 us
    all_to_all x2, waiting for transfers between devices, local(): lax.all_to_all(outgoing.reshape(experts, capacity, hi - lo), 'tp', split_...  106 us
    ppermute x3, waiting for transfers between devices, dp_reduce(): total = total + lax.ppermute(product((here + shift) % ring), 'dp', pairs)  33.4 us
    all_to_all x2, starting transfers between devices, local(): lax.all_to_all(outgoing.reshape(experts, capacity, hi - lo), 'tp', split_...  26 us
    ppermute x3, waiting for transfers between devices, dp_gather(): received.append(lax.ppermute(block, 'dp', pairs))  22.8 us
    all_to_all x1, waiting for transfers between devices, local(): lax.all_to_all(partial.reshape(groups, tok_rows, first), 'dp', split_axis...  12.2 us
    dot_general x4, matrix products, product(): return jnp.dot(rows, weights, preferred_element_type=jnp.float32)  9.24 us
    dot_general x1, matrix products, local(): projected_up = jnp.dot(arrived, gate_up, preferred_element_type=jnp.float32)  9.01 us
  transfers between devices with their start and end apart: 9, of which 7 were waited for; matrix products, arithmetic and copies ran while one was open for 4% of the time, Pallas kernels for 0%

commit v1 on v0

--- a/solution.py
+++ b/solution.py
@@ -36,12 +36,12 @@
 def dp_gather(block):
     ring = lax.axis_size("dp")
     here = lax.axis_index("dp")
-    received = [block]
-    for shift in range(1, ring):
+    gathered = jnp.zeros((ring,) + block.shape, block.dtype)
+    for shift in range(ring):
         pairs = [(j, (j + shift) % ring) for j in range(ring)]
-        received.append(lax.ppermute(block, "dp", pairs))
-    order = (here - jnp.arange(ring, dtype=jnp.int32)) % ring
-    return jnp.take(jnp.stack(received), order, axis=0)
+        piece = block if shift == 0 else lax.ppermute(block, "dp", pairs)
+        gathered = lax.dynamic_update_index_in_dim(gathered, piece, (here - shift) % ring, axis=0)
+    return gathered
 
 
 def local(attn_heads, w_out, residual, moe_gain, router, expert_ids, w_gate_up, w_down, next_gain):

time: 411 us -> 415 us (level)
  blocking collectives: 147 us -> 0 us
  waiting for transfers between devices: 174 us -> 315 us
  matrix products: 33.5 us -> 41.5 us
  starting transfers between devices: 37.2 us -> 43.2 us
  other arithmetic: 14 us -> 9.16 us
    all_to_all x1 -> x0, blocking collectives: 147 us -> none  [local(): lax.all_to_all(served.reshape(experts, capacity, feat_width), 'tp', split...]
    all_to_all x0 -> x1, waiting for transfers between devices: none -> 141 us  [local(): lax.all_to_all(served.reshape(experts, capacity, feat_width), 'tp', split...]
    all_to_all x0 -> x1, starting transfers between devices: none -> 6 us  [local(): lax.all_to_all(served.reshape(experts, capacity, feat_width), 'tp', split...]
  transfers between devices with their start and end apart: 9 -> 10, of which waited for: 7 -> 8; matrix products, arithmetic and copies ran while one was open for 4% -> 4% of each run, Pallas kernels for 0% -> 0%
where the time goes in v1:
time: 415 us; the launch traced here: 414 us
  waiting for transfers between devices  315 us (76%)
  starting transfers between devices  43.2 us (10%)
  matrix products  41.5 us (10%)
  other arithmetic  9.16 us (2%)
  local copies, waits for them, and re-layouts  4.19 us (1%)
    all_to_all x1, waiting for transfers between devices, local(): lax.all_to_all(served.reshape(experts, capacity, feat_width), 'tp', split...  141 us
    all_to_all x2, waiting for transfers between devices, local(): lax.all_to_all(outgoing.reshape(experts, capacity, hi - lo), 'tp', split_...  106 us
    ppermute x3, waiting for transfers between devices, dp_reduce(): total = total + lax.ppermute(product((here + shift) % ring), 'dp', pairs)  33.4 us
    all_to_all x2, starting transfers between devices, local(): lax.all_to_all(outgoing.reshape(experts, capacity, hi - lo), 'tp', split_...  26 us
    ppermute x3, waiting for transfers between devices, dp_gather(): piece = block if shift == 0 else lax.ppermute(block, 'dp', pairs)  22.8 us
    all_to_all x1, waiting for transfers between devices, local(): lax.all_to_all(partial.reshape(groups, tok_rows, first), 'dp', split_axis...  12.2 us
    dot_general x4, matrix products, product(): return jnp.dot(rows, weights, preferred_element_type=jnp.float32)  9.24 us
    dot_general x1, matrix products, local(): projected_up = jnp.dot(arrived, gate_up, preferred_element_type=jnp.float32)  9.01 us
  transfers between devices with their start and end apart: 10, of which 8 were waited for; matrix products, arithmetic and copies ran while one was open for 4% of the time, Pallas kernels for 0%

profile of v1, /device:TPU:1, one launch (start us, length us, event | category | flops | bytes accessed | tf_op | source)
XLA Modules:
  0.0 414.1 jit_solution(10724705807108522339)
XLA Ops:
  0.6 0.0 copy-start
  0.6 0.0 slice-start
  0.7 2.8 fusion.31
  3.4 5.0 %all-to-all-start = ((f32[4,128,512]{2,1,0:T(8,128)}), f32[4,128,512]{2,1,0:T(8,128)S(1)}, u32[]{:S(2)}, u32[]{:S(2)}) async-start(f32[4,128,512]{2,1,0:T(8,128)} %fusion.31), calls=%async_computation | async-start | bytes 2097152 | tf_op jit(solution)/shard_map/all_to_all | solution.py:71
  8.4 0.1 eq.48
  8.6 0.1 convolution_convert_fusion.3
  8.7 1.0 fusion.28
  9.7 12.2 %all-to-all-done = f32[4,128,512]{2,1,0:T(8,128)S(1)} async-done(((f32[4,128,512]{2,1,0:T(8,128)}), f32[4,128,512]{2,1,0:T(8,128)S(1)}, u32[]{:S(2)}, u32[]{:S(2)}) %all-to-all-start) | async-done | bytes 1048608 | tf_op jit(solution)/shard_map/all_to_all | solution.py:71
  21.9 0.8 reduce_sum.72
  22.7 1.0 add_convert_fusion.1
  23.8 2.6 convolution_convert_fusion.2
  26.4 14.2 %all-to-all-start.1 = ((bf16[64,24,512]{2,1,0:T(8,128)(2,1)}), bf16[64,24,512]{2,1,0:T(8,128)(2,1)}, u32[]{:S(2)}, u32[]{:S(2)}) async-start(bf16[64,24,512]{2,1,0:T(8,128)(2,1)} %bitcast.74), calls=%async_computation.1 | async-start | bytes 3145728 | tf_op jit(solution)/shard_map/all_to_all | solution.py:86
  40.6 0.0 copy-start.1
  40.7 2.8 fusion.22
  43.5 0.3 collective-permute-start
  43.8 2.7 fusion.20
  46.4 1.8 collective-permute-start.1
  48.2 1.3 fusion.18
  49.5 0.6 collective-permute-start.2
  50.1 14.1 %collective-permute-done = f32[128,1536]{1,0:T(8,128)} collective-permute-done((f32[128,1536]{1,0:T(8,128)}, f32[128,1536]{1,0:T(8,128)}, u32[]{:S(2)}, u32[]{:S(2)}) %collective-permute-start) | collective-permute-done | bytes 786464 | tf_op jit(solution)/shard_map/ppermute | solution.py:32
  64.2 15.7 %collective-permute-done.1 = f32[128,1536]{1,0:T(8,128)} collective-permute-done((f32[128,1536]{1,0:T(8,128)}, f32[128,1536]{1,0:T(8,128)}, u32[]{:S(2)}, u32[]{:S(2)}) %collective-permute-start.1) | collective-permute-done | bytes 786464 | tf_op jit(solution)/shard_map/ppermute | solution.py:32
  79.9 3.7 collective-permute-done.2
  83.6 2.5 fusion.10
  86.1 0.1 add_convert_fusion
  86.2 3.5 convolution_convert_fusion.1
  89.7 11.8 %all-to-all-start.2 = ((bf16[64,24,1536]{2,1,0:T(8,128)(2,1)}), bf16[64,24,1536]{2,1,0:T(8,128)(2,1)}, u32[]{:S(2)}, u32[]{:S(2)}) async-start(bf16[64,24,1536]{2,1,0:T(8,128)(2,1)} %bitcast.72), calls=%async_computation.2 | async-start | bytes 9437184 | tf_op jit(solution)/shard_map/all_to_all | solution.py:86
  101.5 0.2 fusion.15
  101.7 0.4 fusion.29
  102.2 0.3 fusion.27
  102.5 0.3 fusion.26
  102.8 105.8 %all-to-all-done.2 = bf16[64,24,1536]{2,1,0:T(8,128)(2,1)} async-done(((bf16[64,24,1536]{2,1,0:T(8,128)(2,1)}), bf16[64,24,1536]{2,1,0:T(8,128)(2,1)}, u32[]{:S(2)}, u32[]{:S(2)}) %all-to-all-start.2) | async-done | bytes 4718624 | tf_op jit(solution)/shard_map/all_to_all | solution.py:86
  208.6 4.4 %fusion = f32[1536]{0:T(1024)S(1)} fusion(bf16[1536,1536]{1,0:T(8,128)(2,1)} %bitcast.11, bf16[1536,512]{1,0:T(8,128)(2,1)} %bitcast.9), kind=kLoop, calls=%fused_computation.2 | loop fusion | flops 18872832 | bytes 6297600 | tf_op jit(solution)/shard_map/reduce_sum | solution.py:11
  213.1 9.0 %fusion.3 = f32[1536,1024]{1,0:T(8,128)S(1)} fusion(f32[2048]{0:T(1024)S(1)} %copy-done.9, f32[1536]{0:T(1024)S(1)} %add_rsqrt_fusion, bf16[1,2048,1024]{2,1,0:T(8,128)(2,1)S(1)} %copy-done.7, bf16[1536,1536]{1,0:T(8,128)(2,1)} %bitcast.11, bf16[1536,512]{1,0:T(8,128)(2,1)} %bitcast.9), kind=kOutput, calls=%fused_computation.7 | convolution fusion | flops 6464471040 | bytes 16791552 | tf_op jit(solution)/shard_map/dot_general | solution.py:107
  222.1 5.3 %convolution_convert_fusion = bf16[1536,2048]{1,0:T(8,128)(2,1)} fusion(bf16[1,512,2048]{2,1,0:T(8,128)(2,1)S(1)} %copy-done, f32[1536,1024]{1,0:T(8,128)S(1)} %fusion.3), kind=kOutput, calls=%fused_computation.5 | convolution fusion | flops 3229089792 | bytes 14680064 | tf_op jit(solution)/shard_map/dot_general | solution.py:111
  227.4 6.0 %all-to-all-start.3 = ((bf16[64,24,2048]{2,1,0:T(8,128)(2,1)}), bf16[64,24,2048]{2,1,0:T(8,128)(2,1)}, u32[]{:S(2)}, u32[]{:S(2)}) async-start(bf16[64,24,2048]{2,1,0:T(8,128)(2,1)} %bitcast.73), calls=%async_computation.3 | async-start | bytes 12582912 | tf_op jit(solution)/shard_map/all_to_all | solution.py:114
  233.4 140.8 %all-to-all-done.3 = bf16[64,24,2048]{2,1,0:T(8,128)(2,1)} async-done(((bf16[64,24,2048]{2,1,0:T(8,128)(2,1)}), bf16[64,24,2048]{2,1,0:T(8,128)(2,1)}, u32[]{:S(2)}, u32[]{:S(2)}) %all-to-all-start.3) | async-done | bytes 6291488 | tf_op jit(solution)/shard_map/all_to_all | solution.py:114
  374.2 3.8 fusion.52
  378.1 0.0 copy-start.6
  378.1 4.7 %multiply_reduce_fusion = (f32[128]{0:T(128)S(1)}, bf16[128,2048]{1,0:T(8,128)(2,1)}, f32[128,2048]{1,0:T(8,128)S(1)}) fusion(f32[128,2048]{1,0:T(8,128)S(1)} %fusion.52, bf16[1536,128]{1,0:T(8,128)(2,1)S(1)} %fusion.27, bf16[1536,2048]{1,0:T(8,128)(2,1)} %bitcast.17, bf16[128,1536]{1,0:T(8,128)(2,1)S(1)} %add_convert_fusion, ...), kind=kOutput, calls=%fused_computation.29 | convolution fusion | flops 807665536 | bytes 9830912 | tf_op jit(solution)/shard_map/dot_general | solution.py:120
  382.7 0.2 broadcast_in_dim.75
  383.0 1.0 bitcast_dynamic-update-slice_fusion.3
  384.0 1.3 copy-done.2
  385.3 3.5 collective-permute-start.4
  388.8 11.5 %collective-permute-done.3 = bf16[128,2048]{1,0:T(8,128)(2,1)S(1)} collective-permute-done((bf16[128,2048]{1,0:T(8,128)(2,1)}, bf16[128,2048]{1,0:T(8,128)(2,1)S(1)}, u32[]{:S(2)}, u32[]{:S(2)}) %collective-permute-start.3) | collective-permute-done | bytes 524320 | tf_op jit(solution)/shard_map/ppermute | solution.py:42
  400.3 0.8 bitcast_dynamic-update-slice_fusion.2
  401.1 11.3 %collective-permute-done.4 = bf16[128,2048]{1,0:T(8,128)(2,1)S(1)} collective-permute-done((bf16[128,2048]{1,0:T(8,128)(2,1)}, bf16[128,2048]{1,0:T(8,128)(2,1)S(1)}, u32[]{:S(2)}, u32[]{:S(2)}) %collective-permute-start.4) | collective-permute-done | bytes 524320 | tf_op jit(solution)/shard_map/ppermute | solution.py:42
  412.4 0.8 bitcast_dynamic-update-slice_fusion.1
  413.2 0.8 bitcast_dynamic-update-slice_fusion
  (33 shorter events, 0.2 us)
Async XLA Ops:
  0.6 221.4 %copy-start = (bf16[1,512,2048]{2,1,0:T(8,128)(2,1)S(1)}, bf16[1,512,2048]{2,1,0:T(8,128)(2,1)}, u32[]{:S(2)}) copy-start(bf16[1,512,2048]{2,1,0:T(8,128)(2,1)} %param.16) | copy-start | bytes 6291460
  0.6 22.1 %slice-start = ((bf16[128,2048]{1,0:T(8,128)(2,1)}), bf16[128,512]{1,0:T(8,128)(2,1)S(1)}, s32[]{:S(2)}) async-start(bf16[128,2048]{1,0:T(8,128)(2,1)} %param.11), calls=%async_computation.4 | async-start | bytes 262144 | tf_op jit(solution)/shard_map/slice | solution.py:78
  0.7 7.9 %copy-start.5 = (s32[128,8]{0,1:T(8,128)S(1)}, s32[128,8]{0,1:T(8,128)}, u32[]{:S(2)}) copy-start(s32[128,8]{0,1:T(8,128)} %param.14) | copy-start | bytes 12292
  3.4 18.5 %all-to-all-start = ((f32[4,128,512]{2,1,0:T(8,128)}), f32[4,128,512]{2,1,0:T(8,128)S(1)}, u32[]{:S(2)}, u32[]{:S(2)}) async-start(f32[4,128,512]{2,1,0:T(8,128)} %fusion.31), calls=%async_computation | async-start | bytes 2097152 | tf_op jit(solution)/shard_map/all_to_all | solution.py:71
  22.7 17.9 %copy-start.3 = (bf16[4,128,512]{2,1,0:T(8,128)(2,1)S(1)}, bf16[4,128,512]{2,1,0:T(8,128)(2,1)}, u32[]{:S(2)}) copy-start(bf16[4,128,512]{2,1,0:T(8,128)(2,1)} %param.9) | copy-start | bytes 1572868
  26.4 63.3 %all-to-all-start.1 = ((bf16[64,24,512]{2,1,0:T(8,128)(2,1)}), bf16[64,24,512]{2,1,0:T(8,128)(2,1)}, u32[]{:S(2)}, u32[]{:S(2)}) async-start(bf16[64,24,512]{2,1,0:T(8,128)(2,1)} %bitcast.74), calls=%async_computation.1 | async-start | bytes 3145728 | tf_op jit(solution)/shard_map/all_to_all | solution.py:86
  40.6 7.6 %copy-start.1 = (bf16[512,2048]{1,0:T(8,128)(2,1)S(1)}, bf16[512,2048]{1,0:T(8,128)(2,1)}, u32[]{:S(2)}) copy-start(bf16[512,2048]{1,0:T(8,128)(2,1)} %param.10) | copy-start | bytes 6291460
  43.5 20.7 %collective-permute-start = (f32[128,1536]{1,0:T(8,128)}, f32[128,1536]{1,0:T(8,128)}, u32[]{:S(2)}, u32[]{:S(2)}) collective-permute-start(f32[128,1536]{1,0:T(8,128)} %fusion.22), channel_id=1, source_target_pairs={{0,64},{64,128},{128,192},{192,0},{1,65},{65,129},{129,193},{193,1... | collective-permute-start | bytes 2359304 | tf_op jit(solution)/shard_map/ppermute | solution.py:32
  46.4 33.4 %collective-permute-start.1 = (f32[128,1536]{1,0:T(8,128)}, f32[128,1536]{1,0:T(8,128)}, u32[]{:S(2)}, u32[]{:S(2)}) collective-permute-start(f32[128,1536]{1,0:T(8,128)} %fusion.20), channel_id=1, source_target_pairs={{0,128},{64,192},{128,0},{192,64},{1,129},{65,193},{129,1},{193,65... | collective-permute-start | bytes 2359304 | tf_op jit(solution)/shard_map/ppermute | solution.py:32
  49.5 36.5 %slice-start.1 = ((bf16[128,2048]{1,0:T(8,128)(2,1)}), bf16[128,1536]{1,0:T(8,128)(2,1)S(1)}, s32[]{:S(2)}) async-start(bf16[128,2048]{1,0:T(8,128)(2,1)} %param.11), calls=%async_computation.5 | async-start | bytes 786432 | tf_op jit(solution)/shard_map/slice | solution.py:78
  49.5 34.1 %collective-permute-start.2 = (f32[128,1536]{1,0:T(8,128)}, f32[128,1536]{1,0:T(8,128)}, u32[]{:S(2)}, u32[]{:S(2)}) collective-permute-start(f32[128,1536]{1,0:T(8,128)} %fusion.18), channel_id=1, source_target_pairs={{0,192},{64,0},{128,64},{192,128},{1,193},{65,1},{129,65},{193,129... | collective-permute-start | bytes 2359304 | tf_op jit(solution)/shard_map/ppermute | solution.py:32
  50.1 36.0 %copy-start.4 = (pred[1536,128]{1,0:T(32,128)(4,1)S(1)}, pred[1536,128]{1,0:T(32,128)(4,1)}, u32[]{:S(2)}) copy-start(pred[1536,128]{1,0:T(32,128)(4,1)} %fusion.28) | copy-start | bytes 589828
  89.7 12.0 %copy-start.8 = (bf16[2048,64]{0,1:T(8,128)(2,1)S(1)}, bf16[2048,64]{0,1:T(8,128)(2,1)}, u32[]{:S(2)}) copy-start(bf16[2048,64]{0,1:T(8,128)(2,1)} %param.13) | copy-start | bytes 786436
  89.7 12.0 %copy-start.9 = (f32[2048]{0:T(1024)S(1)}, f32[2048]{0:T(1024)}, u32[]{:S(2)}) copy-start(f32[2048]{0:T(1024)} %param.12) | copy-start | bytes 24580
  89.7 118.9 %all-to-all-start.2 = ((bf16[64,24,1536]{2,1,0:T(8,128)(2,1)}), bf16[64,24,1536]{2,1,0:T(8,128)(2,1)}, u32[]{:S(2)}, u32[]{:S(2)}) async-start(bf16[64,24,1536]{2,1,0:T(8,128)(2,1)} %bitcast.72), calls=%async_computation.2 | async-start | bytes 9437184 | tf_op jit(solution)/shard_map/all_to_all | solution.py:86
  208.6 4.4 %copy-start.7 = (bf16[1,2048,1024]{2,1,0:T(8,128)(2,1)S(1)}, bf16[1,2048,1024]{2,1,0:T(8,128)(2,1)}, u32[]{:S(2)}) copy-start(bf16[1,2048,1024]{2,1,0:T(8,128)(2,1)} %param.15) | copy-start | bytes 12582916
  227.4 146.8 %all-to-all-start.3 = ((bf16[64,24,2048]{2,1,0:T(8,128)(2,1)}), bf16[64,24,2048]{2,1,0:T(8,128)(2,1)}, u32[]{:S(2)}, u32[]{:S(2)}) async-start(bf16[64,24,2048]{2,1,0:T(8,128)(2,1)} %bitcast.73), calls=%async_computation.3 | async-start | bytes 12582912 | tf_op jit(solution)/shard_map/all_to_all | solution.py:114
  378.1 4.9 %copy-start.6 = (f32[2048]{0:T(1024)S(1)}, f32[2048]{0:T(1024)}, u32[]{:S(2)}) copy-start(f32[2048]{0:T(1024)} %param.17) | copy-start | bytes 24580
  384.0 1.3 copy-start.2
  385.3 15.0 %collective-permute-start.3 = (bf16[128,2048]{1,0:T(8,128)(2,1)}, bf16[128,2048]{1,0:T(8,128)(2,1)S(1)}, u32[]{:S(2)}, u32[]{:S(2)}) collective-permute-start(bf16[128,2048]{1,0:T(8,128)(2,1)} %get-tuple-element.21), channel_id=1, source_target_pairs={{0,64},{64,128},{128,192},{192,0},{1,65},{65,129},{129,193},{193,1... | collective-permute-start | bytes 1572872 | tf_op jit(solution)/shard_map/ppermute | solution.py:42
  385.3 27.1 %collective-permute-start.4 = (bf16[128,2048]{1,0:T(8,128)(2,1)}, bf16[128,2048]{1,0:T(8,128)(2,1)S(1)}, u32[]{:S(2)}, u32[]{:S(2)}) collective-permute-start(bf16[128,2048]{1,0:T(8,128)(2,1)} %get-tuple-element.21), channel_id=1, source_target_pairs={{0,128},{64,192},{128,0},{192,64},{1,129},{65,193},{129,1},{193,65... | collective-permute-start | bytes 1572872 | tf_op jit(solution)/shard_map/ppermute | solution.py:42
  388.8 24.4 %collective-permute-start.5 = (bf16[128,2048]{1,0:T(8,128)(2,1)}, bf16[128,2048]{1,0:T(8,128)(2,1)S(1)}, u32[]{:S(2)}, u32[]{:S(2)}) collective-permute-start(bf16[128,2048]{1,0:T(8,128)(2,1)} %get-tuple-element.21), channel_id=1, source_target_pairs={{0,192},{64,0},{128,64},{192,128},{1,193},{65,1},{129,65},{193,129... | collective-permute-start | bytes 1572872 | tf_op jit(solution)/shard_map/ppermute | solution.py:42

commit v2 on v1

--- a/solution.py
+++ b/solution.py
@@ -33,17 +33,6 @@
     return total
 
 
-def dp_gather(block):
-    ring = lax.axis_size("dp")
-    here = lax.axis_index("dp")
-    gathered = jnp.zeros((ring,) + block.shape, block.dtype)
-    for shift in range(ring):
-        pairs = [(j, (j + shift) % ring) for j in range(ring)]
-        piece = block if shift == 0 else lax.ppermute(block, "dp", pairs)
-        gathered = lax.dynamic_update_index_in_dim(gathered, piece, (here - shift) % ring, axis=0)
-    return gathered
-
-
 def local(attn_heads, w_out, residual, moe_gain, router, expert_ids, w_gate_up, w_down, next_gain):
     groups, tok_rows, quarter = attn_heads.shape
     feat_width = w_out.shape[1]
@@ -65,7 +54,7 @@
     dispatch = placed.reshape(slots, tok_rows).astype(jnp.bfloat16)
 
     first = feat_width // 4
-    bounds = [(0, first), (first, feat_width)]
+    bounds = [(0, first), (first, 2 * first), (2 * first, feat_width)]
     flat_heads = attn_heads.reshape(groups * tok_rows, quarter)
     partial = jnp.dot(flat_heads, w_out[:, :first], preferred_element_type=jnp.float32)
     pieces = lax.all_to_all(
@@ -79,9 +68,10 @@
         mid_c = (res_c.astype(jnp.float32) + part).astype(jnp.bfloat16)
         mid_parts.append(mid_c)
         outgoing = jnp.dot(dispatch, mid_c, preferred_element_type=jnp.float32).astype(jnp.bfloat16)
-        if c == 0:
+        if c + 1 < len(bounds):
             outgoing, heads_now = lax.optimization_barrier((outgoing, attn_heads))
-            part = dp_reduce(heads_now, w_out[:, first:])
+            next_lo, next_hi = bounds[c + 1]
+            part = dp_reduce(heads_now, w_out[:, next_lo:next_hi])
         arrived_parts.append(
             lax.all_to_all(
                 outgoing.reshape(experts, capacity, hi - lo), "tp", split_axis=0, concat_axis=0, tiled=True
@@ -122,7 +112,8 @@
     layer_sum = mid_wide + expert_sum
     layer_out = layer_sum.astype(jnp.bfloat16)
     next_local = rms_scale(layer_sum, next_gain).astype(jnp.bfloat16)
-    next_input = dp_gather(next_local)
+    copies = jnp.broadcast_to(next_local[None], (groups, tok_rows, feat_width))
+    next_input = lax.all_to_all(copies, "dp", split_axis=0, concat_axis=0, tiled=True)
     return (layer_out, next_input)
 
 

time: 415 us -> 403 us (0.971)
  blocking collectives: 0 us -> 175 us
  waiting for transfers between devices: 315 us -> 142 us
  matrix products: 41.5 us -> 34.9 us
  starting transfers between devices: 43.2 us -> 37.5 us
    all_to_all x0 -> x2, blocking collectives: none -> 175 us  [the longest x1 147 us: local(): lax.all_to_all(served.reshape(experts, capacity, feat_width), 'tp', split...]
    all_to_all x1 -> x0, waiting for transfers between devices: 141 us -> none  [local(): lax.all_to_all(served.reshape(experts, capacity, feat_width), 'tp', split...]
    ppermute x3 -> x0, waiting for transfers between devices: 22.8 us -> none  [dp_gather(): piece = block if shift == 0 else lax.ppermute(block, 'dp', pairs)]
    all_to_all x2 -> x3, waiting for transfers between devices: 106 us -> 95.5 us  [local(): lax.all_to_all(outgoing.reshape(experts, capacity, hi - lo), 'tp', split_...]
    all_to_all x1 -> x0, starting transfers between devices: 6 us -> none  [local(): lax.all_to_all(served.reshape(experts, capacity, feat_width), 'tp', split...]
    ppermute x3 -> x6, waiting for transfers between devices: 33.4 us -> 35.3 us  [dp_reduce(): total = total + lax.ppermute(product((here + shift) % ring), 'dp', pairs)]
    dot_general x4 -> x8, matrix products: 9.24 us -> 10.6 us  [product(): return jnp.dot(rows, weights, preferred_element_type=jnp.float32)]
    all_to_all x2 -> x3, starting transfers between devices: 26 us -> 27 us  [local(): lax.all_to_all(outgoing.reshape(experts, capacity, hi - lo), 'tp', split_...]
  transfers between devices with their start and end apart: 10 -> 10, of which waited for: 8 -> 10; matrix products, arithmetic and copies ran while one was open for 4% -> 5% of each run, Pallas kernels for 0% -> 0%
where the time goes in v2:
time: 403 us; the launch traced here: 402 us
  blocking collectives  175 us (43%)
  waiting for transfers between devices  142 us (35%)
  starting transfers between devices  37.5 us (9%)
  matrix products  34.9 us (9%)
  other arithmetic  8.54 us (2%)
    all_to_all x1, blocking collectives, local(): lax.all_to_all(served.reshape(experts, capacity, feat_width), 'tp', split...  147 us
    all_to_all x3, waiting for transfers between devices, local(): lax.all_to_all(outgoing.reshape(experts, capacity, hi - lo), 'tp', split_...  95.5 us
    ppermute x6, waiting for transfers between devices, dp_reduce(): total = total + lax.ppermute(product((here + shift) % ring), 'dp', pairs)  35.3 us
    all_to_all x1, blocking collectives, local(): lax.all_to_all(copies, 'dp', split_axis=0, concat_axis=0, tiled=True)  28.5 us
    all_to_all x3, starting transfers between devices, local(): lax.all_to_all(outgoing.reshape(experts, capacity, hi - lo), 'tp', split_...  27 us
    all_to_all x1, waiting for transfers between devices, local(): lax.all_to_all(partial.reshape(groups, tok_rows, first), 'dp', split_axis...  11.2 us
    dot_general x8, matrix products, product(): return jnp.dot(rows, weights, preferred_element_type=jnp.float32)  10.6 us
    dot_general x1, matrix products, local(): projected_up = jnp.dot(arrived, gate_up, preferred_element_type=jnp.float32)  9.11 us
  transfers between devices with their start and end apart: 10, of which 10 were waited for; matrix products, arithmetic and copies ran while one was open for 5% of the time, Pallas kernels for 0%

profile of v2, /device:TPU:1, one launch (start us, length us, event | category | flops | bytes accessed | tf_op | source)
XLA Modules:
  0.0 402.5 jit_solution(2046514655721248994)
XLA Ops:
  0.7 2.8 fusion.33
  3.4 5.0 %all-to-all-start = ((f32[4,128,512]{2,1,0:T(8,128)}), f32[4,128,512]{2,1,0:T(8,128)S(1)}, u32[]{:S(2)}, u32[]{:S(2)}) async-start(f32[4,128,512]{2,1,0:T(8,128)} %fusion.33), calls=%async_computation | async-start | bytes 2097152 | tf_op jit(solution)/shard_map/all_to_all | solution.py:60
  8.7 0.3 fusion.23
  9.0 1.7 fusion.72
  10.7 11.2 %all-to-all-done = f32[4,128,512]{2,1,0:T(8,128)S(1)} async-done(((f32[4,128,512]{2,1,0:T(8,128)}), f32[4,128,512]{2,1,0:T(8,128)S(1)}, u32[]{:S(2)}, u32[]{:S(2)}) %all-to-all-start) | async-done | bytes 1048608 | tf_op jit(solution)/shard_map/all_to_all | solution.py:60
  21.9 0.8 reduce_sum.72
  22.7 1.1 add_convert_fusion.2
  23.8 1.7 convolution_convert_fusion.3
  25.5 14.3 %all-to-all-start.1 = ((bf16[64,24,512]{2,1,0:T(8,128)(2,1)}), bf16[64,24,512]{2,1,0:T(8,128)(2,1)}, u32[]{:S(2)}, u32[]{:S(2)}) async-start(bf16[64,24,512]{2,1,0:T(8,128)(2,1)} %bitcast.84), calls=%async_computation.1 | async-start | bytes 3145728 | tf_op jit(solution)/shard_map/all_to_all | solution.py:76
  39.9 1.3 fusion.38
  41.2 2.0 fusion.40
  43.1 2.0 fusion.42
  45.1 0.3 collective-permute-start
  45.4 1.8 collective-permute-start.1
  47.2 0.6 collective-permute-start.2
  47.8 6.8 %collective-permute-done = f32[128,512]{1,0:T(8,128)} collective-permute-done((f32[128,512]{1,0:T(8,128)}, f32[128,512]{1,0:T(8,128)}, u32[]{:S(2)}, u32[]{:S(2)}) %collective-permute-start) | collective-permute-done | bytes 262176 | tf_op jit(solution)/shard_map/ppermute | solution.py:32
  54.6 4.5 %collective-permute-done.1 = f32[128,512]{1,0:T(8,128)} collective-permute-done((f32[128,512]{1,0:T(8,128)}, f32[128,512]{1,0:T(8,128)}, u32[]{:S(2)}, u32[]{:S(2)}) %collective-permute-start.1) | collective-permute-done | bytes 262176 | tf_op jit(solution)/shard_map/ppermute | solution.py:32
  59.1 0.9 collective-permute-done.2
  60.0 1.5 fusion.16
  61.6 1.7 convolution_convert_fusion.2
  63.3 16.3 %all-to-all-done.1 = bf16[64,24,512]{2,1,0:T(8,128)(2,1)} async-done(((bf16[64,24,512]{2,1,0:T(8,128)(2,1)}), bf16[64,24,512]{2,1,0:T(8,128)(2,1)}, u32[]{:S(2)}, u32[]{:S(2)}) %all-to-all-start.1) | async-done | bytes 1572896 | tf_op jit(solution)/shard_map/all_to_all | solution.py:76
  79.5 6.3 %all-to-all-start.2 = ((bf16[64,24,512]{2,1,0:T(8,128)(2,1)}), bf16[64,24,512]{2,1,0:T(8,128)(2,1)}, u32[]{:S(2)}, u32[]{:S(2)}) async-start(bf16[64,24,512]{2,1,0:T(8,128)(2,1)} %bitcast.85), calls=%async_computation.2 | async-start | bytes 3145728 | tf_op jit(solution)/shard_map/all_to_all | solution.py:76
  85.8 1.7 fusion.24
  87.5 1.5 fusion.26
  89.1 0.3 fusion.28
  89.4 0.4 collective-permute-start.3
  89.7 1.8 collective-permute-start.4
  91.5 0.7 collective-permute-start.5
  92.2 12.1 %collective-permute-done.3 = f32[128,1024]{1,0:T(8,128)S(1)} collective-permute-done((f32[128,1024]{1,0:T(8,128)S(1)}, f32[128,1024]{1,0:T(8,128)S(1)}, u32[]{:S(2)}, u32[]{:S(2)}) %collective-permute-start.3) | collective-permute-done | bytes 524320 | tf_op jit(solution)/shard_map/ppermute | solution.py:32
  104.3 10.1 %collective-permute-done.4 = f32[128,1024]{1,0:T(8,128)S(1)} collective-permute-done((f32[128,1024]{1,0:T(8,128)S(1)}, f32[128,1024]{1,0:T(8,128)S(1)}, u32[]{:S(2)}, u32[]{:S(2)}) %collective-permute-start.4) | collective-permute-done | bytes 524320 | tf_op jit(solution)/shard_map/ppermute | solution.py:32
  114.4 0.9 collective-permute-done.5
  115.4 0.3 fusion.14
  115.7 2.7 convolution_convert_fusion.1
  118.4 7.1 %all-to-all-done.2 = bf16[64,24,512]{2,1,0:T(8,128)(2,1)} async-done(((bf16[64,24,512]{2,1,0:T(8,128)(2,1)}), bf16[64,24,512]{2,1,0:T(8,128)(2,1)}, u32[]{:S(2)}, u32[]{:S(2)}) %all-to-all-start.2) | async-done | bytes 1572896 | tf_op jit(solution)/shard_map/all_to_all | solution.py:76
  125.5 6.4 %all-to-all-start.3 = ((bf16[64,24,1024]{2,1,0:T(8,128)(2,1)}), bf16[64,24,1024]{2,1,0:T(8,128)(2,1)}, u32[]{:S(2)}, u32[]{:S(2)}) async-start(bf16[64,24,1024]{2,1,0:T(8,128)(2,1)} %bitcast.82), calls=%async_computation.3 | async-start | bytes 6291456 | tf_op jit(solution)/shard_map/all_to_all | solution.py:76
  132.1 0.4 fusion.31
  132.6 0.3 fusion.22
  132.9 0.3 fusion.21
  133.2 72.1 %all-to-all-done.3 = bf16[64,24,1024]{2,1,0:T(8,128)(2,1)} async-done(((bf16[64,24,1024]{2,1,0:T(8,128)(2,1)}), bf16[64,24,1024]{2,1,0:T(8,128)(2,1)}, u32[]{:S(2)}, u32[]{:S(2)}) %all-to-all-start.3) | async-done | bytes 3145760 | tf_op jit(solution)/shard_map/all_to_all | solution.py:76
  205.3 4.4 %fusion = f32[1536]{0:T(1024)S(1)} fusion(bf16[1536,1024]{1,0:T(8,128)(2,1)} %bitcast.17, bf16[1536,512]{1,0:T(8,128)(2,1)} %bitcast.15, bf16[1536,512]{1,0:T(8,128)(2,1)} %bitcast.13), kind=kLoop, calls=%fused_computation.2 | loop fusion | flops 25164288 | bytes 6297600 | tf_op jit(solution)/shard_map/reduce_sum | solution.py:11
  209.7 9.1 %fusion.3 = f32[1536,1024]{1,0:T(8,128)S(1)} fusion(f32[2048]{0:T(1024)S(1)} %copy-done.10, f32[1536]{0:T(1024)S(1)} %add_rsqrt_fusion, bf16[1,2048,1024]{2,1,0:T(8,128)(2,1)S(1)} %copy-done.8, bf16[1536,1024]{1,0:T(8,128)(2,1)} %bitcast.17, bf16[1536,512]{1,0:T(8,128)(2,1)} %bitcast.15, bf16[1536,512]{1,0:T(8,128)(2,1)} %bitcast.13), kind=kOutput, calls=%fused_computation.6 | convolution fusion | flops 6470762496 | bytes 16791552 | tf_op jit(solution)/shard_map/dot_general | solution.py:97
  218.9 3.7 convolution_convert_fusion
  222.5 146.6 %all_to_all.30 = bf16[64,24,2048]{2,1,0:T(8,128)(2,1)S(1)} all-to-all(bf16[64,24,2048]{2,1,0:T(8,128)(2,1)S(1)} %bitcast.83), channel_id=1, replica_groups=mesh['dp'=4,'tp'=64] {'tp'}, dimensions={0} | all-to-all | bytes 12582912 | tf_op jit(solution)/shard_map/all_to_all | solution.py:104
  369.2 1.0 fusion.73
  370.2 1.1 multiply_reduce_fusion
  371.4 1.0 multiply_convert_fusion
  372.7 28.5 %all_to_all.31 = bf16[4,128,2048]{2,1,0:T(8,128)(2,1)S(1)} all-to-all(bf16[4,128,2048]{2,1,0:T(8,128)(2,1)S(1)} %broadcast_in_dim.44), channel_id=1, replica_groups=mesh['dp'=4,'tp'=64] {'dp'}, dimensions={0} | all-to-all | bytes 4194304 | tf_op jit(solution)/shard_map/all_to_all | solution.py:116
  401.2 1.3 copy.22
  (40 shorter events, 1.0 us)
Async XLA Ops:
  0.6 218.2 %copy-start = (bf16[1,512,2048]{2,1,0:T(8,128)(2,1)S(1)}, bf16[1,512,2048]{2,1,0:T(8,128)(2,1)}, u32[]{:S(2)}) copy-start(bf16[1,512,2048]{2,1,0:T(8,128)(2,1)} %param.16) | copy-start | bytes 6291460
  0.6 7.9 %copy-start.6 = (s32[128,8]{0,1:T(8,128)S(1)}, s32[128,8]{0,1:T(8,128)}, u32[]{:S(2)}) copy-start(s32[128,8]{0,1:T(8,128)} %param.14) | copy-start | bytes 12292
  3.4 18.5 %all-to-all-start = ((f32[4,128,512]{2,1,0:T(8,128)}), f32[4,128,512]{2,1,0:T(8,128)S(1)}, u32[]{:S(2)}, u32[]{:S(2)}) async-start(f32[4,128,512]{2,1,0:T(8,128)} %fusion.33), calls=%async_computation | async-start | bytes 2097152 | tf_op jit(solution)/shard_map/all_to_all | solution.py:60
  22.7 17.2 %copy-start.2 = (bf16[4,128,512]{2,1,0:T(8,128)(2,1)S(1)}, bf16[4,128,512]{2,1,0:T(8,128)(2,1)}, u32[]{:S(2)}) copy-start(bf16[4,128,512]{2,1,0:T(8,128)(2,1)} %param.9) | copy-start | bytes 1572868
  25.5 36.0 %copy-start.5 = (bf16[128,512]{1,0:T(8,128)(2,1)S(1)}, bf16[128,512]{1,0:T(8,128)(2,1)}, u32[]{:S(2)}) copy-start(bf16[128,512]{1,0:T(8,128)(2,1)} %get-tuple-element.18) | copy-start | bytes 393220
  25.5 54.0 %all-to-all-start.1 = ((bf16[64,24,512]{2,1,0:T(8,128)(2,1)}), bf16[64,24,512]{2,1,0:T(8,128)(2,1)}, u32[]{:S(2)}, u32[]{:S(2)}) async-start(bf16[64,24,512]{2,1,0:T(8,128)(2,1)} %bitcast.84), calls=%async_computation.1 | async-start | bytes 3145728 | tf_op jit(solution)/shard_map/all_to_all | solution.py:76
  45.1 9.5 %collective-permute-start = (f32[128,512]{1,0:T(8,128)}, f32[128,512]{1,0:T(8,128)}, u32[]{:S(2)}, u32[]{:S(2)}) collective-permute-start(f32[128,512]{1,0:T(8,128)} %fusion.42), channel_id=1, source_target_pairs={{0,64},{64,128},{128,192},{192,0},{1,65},{65,129},{129,193},{193,1... | collective-permute-start | bytes 786440 | tf_op jit(solution)/shard_map/ppermute | solution.py:32
  45.4 13.6 %collective-permute-start.1 = (f32[128,512]{1,0:T(8,128)}, f32[128,512]{1,0:T(8,128)}, u32[]{:S(2)}, u32[]{:S(2)}) collective-permute-start(f32[128,512]{1,0:T(8,128)} %fusion.40), channel_id=1, source_target_pairs={{0,128},{64,192},{128,0},{192,64},{1,129},{65,193},{129,1},{193,65... | collective-permute-start | bytes 786440 | tf_op jit(solution)/shard_map/ppermute | solution.py:32
  47.2 12.8 %collective-permute-start.2 = (f32[128,512]{1,0:T(8,128)S(1)}, f32[128,512]{1,0:T(8,128)}, u32[]{:S(2)}, u32[]{:S(2)}) collective-permute-start(f32[128,512]{1,0:T(8,128)S(1)} %fusion.38), channel_id=1, source_target_pairs={{0,192},{64,0},{128,64},{192,128},{1,193},{65,1},{129,65},{193,129... | collective-permute-start | bytes 786440 | tf_op jit(solution)/shard_map/ppermute | solution.py:32
  61.6 70.6 %copy-start.3 = (bf16[128,512]{1,0:T(8,128)(2,1)}, bf16[128,512]{1,0:T(8,128)(2,1)S(1)}, u32[]{:S(2)}) copy-start(bf16[128,512]{1,0:T(8,128)(2,1)S(1)} %add_convert_fusion.1) | copy-start | bytes 393220
  79.5 46.0 %all-to-all-start.2 = ((bf16[64,24,512]{2,1,0:T(8,128)(2,1)}), bf16[64,24,512]{2,1,0:T(8,128)(2,1)}, u32[]{:S(2)}, u32[]{:S(2)}) async-start(bf16[64,24,512]{2,1,0:T(8,128)(2,1)} %bitcast.85), calls=%async_computation.2 | async-start | bytes 3145728 | tf_op jit(solution)/shard_map/all_to_all | solution.py:76
  85.8 3.2 copy-start.1
  89.1 26.6 %slice-start = ((bf16[128,2048]{1,0:T(8,128)(2,1)}), bf16[128,1024]{1,0:T(8,128)(2,1)S(1)}, s32[]{:S(2)}) async-start(bf16[128,2048]{1,0:T(8,128)(2,1)} %param.11), calls=%async_computation.6 | async-start | bytes 524288 | tf_op jit(solution)/shard_map/slice | solution.py:67
  89.4 14.9 %collective-permute-start.3 = (f32[128,1024]{1,0:T(8,128)S(1)}, f32[128,1024]{1,0:T(8,128)S(1)}, u32[]{:S(2)}, u32[]{:S(2)}) collective-permute-start(f32[128,1024]{1,0:T(8,128)S(1)} %fusion.28), channel_id=1, source_target_pairs={{0,64},{64,128},{128,192},{192,0},{1,65},{65,129},{129,193},{193,1... | collective-permute-start | bytes 1572872 | tf_op jit(solution)/shard_map/ppermute | solution.py:32
  89.7 24.7 %collective-permute-start.4 = (f32[128,1024]{1,0:T(8,128)S(1)}, f32[128,1024]{1,0:T(8,128)S(1)}, u32[]{:S(2)}, u32[]{:S(2)}) collective-permute-start(f32[128,1024]{1,0:T(8,128)S(1)} %fusion.26), channel_id=1, source_target_pairs={{0,128},{64,192},{128,0},{192,64},{1,129},{65,193},{129,1},{193,65... | collective-permute-start | bytes 1572872 | tf_op jit(solution)/shard_map/ppermute | solution.py:32
  91.5 23.8 %collective-permute-start.5 = (f32[128,1024]{1,0:T(8,128)S(1)}, f32[128,1024]{1,0:T(8,128)S(1)}, u32[]{:S(2)}, u32[]{:S(2)}) collective-permute-start(f32[128,1024]{1,0:T(8,128)S(1)} %fusion.24), channel_id=1, source_target_pairs={{0,192},{64,0},{128,64},{192,128},{1,193},{65,1},{129,65},{193,129... | collective-permute-start | bytes 1572872 | tf_op jit(solution)/shard_map/ppermute | solution.py:32
  125.5 6.6 %copy-start.9 = (bf16[2048,64]{0,1:T(8,128)(2,1)S(1)}, bf16[2048,64]{0,1:T(8,128)(2,1)}, u32[]{:S(2)}) copy-start(bf16[2048,64]{0,1:T(8,128)(2,1)} %param.13) | copy-start | bytes 786436
  125.5 6.6 %copy-start.10 = (f32[2048]{0:T(1024)S(1)}, f32[2048]{0:T(1024)}, u32[]{:S(2)}) copy-start(f32[2048]{0:T(1024)} %param.12) | copy-start | bytes 24580
  125.5 79.8 %all-to-all-start.3 = ((bf16[64,24,1024]{2,1,0:T(8,128)(2,1)}), bf16[64,24,1024]{2,1,0:T(8,128)(2,1)}, u32[]{:S(2)}, u32[]{:S(2)}) async-start(bf16[64,24,1024]{2,1,0:T(8,128)(2,1)} %bitcast.82), calls=%async_computation.3 | async-start | bytes 6291456 | tf_op jit(solution)/shard_map/all_to_all | solution.py:76
  205.3 4.4 %copy-start.8 = (bf16[1,2048,1024]{2,1,0:T(8,128)(2,1)S(1)}, bf16[1,2048,1024]{2,1,0:T(8,128)(2,1)}, u32[]{:S(2)}) copy-start(bf16[1,2048,1024]{2,1,0:T(8,128)(2,1)} %param.15) | copy-start | bytes 12582916
  369.2 1.0 copy-start.4
  370.2 1.2 copy-start.7

commit v3 on v2

--- a/solution.py
+++ b/solution.py
@@ -54,7 +54,7 @@
     dispatch = placed.reshape(slots, tok_rows).astype(jnp.bfloat16)
 
     first = feat_width // 4
-    bounds = [(0, first), (first, 2 * first), (2 * first, feat_width)]
+    bounds = [(0, first), (first, feat_width)]
     flat_heads = attn_heads.reshape(groups * tok_rows, quarter)
     partial = jnp.dot(flat_heads, w_out[:, :first], preferred_element_type=jnp.float32)
     pieces = lax.all_to_all(
@@ -68,10 +68,9 @@
         mid_c = (res_c.astype(jnp.float32) + part).astype(jnp.bfloat16)
         mid_parts.append(mid_c)
         outgoing = jnp.dot(dispatch, mid_c, preferred_element_type=jnp.float32).astype(jnp.bfloat16)
-        if c + 1 < len(bounds):
+        if c == 0:
             outgoing, heads_now = lax.optimization_barrier((outgoing, attn_heads))
-            next_lo, next_hi = bounds[c + 1]
-            part = dp_reduce(heads_now, w_out[:, next_lo:next_hi])
+            part = dp_reduce(heads_now, w_out[:, first:])
         arrived_parts.append(
             lax.all_to_all(
                 outgoing.reshape(experts, capacity, hi - lo), "tp", split_axis=0, concat_axis=0, tiled=True
@@ -88,13 +87,20 @@
     combine = jnp.where(placed, weight_full.T[:, None, :], 0.0).reshape(slots, tok_rows)
     combine_hi, combine_lo = split_hi_lo(combine)
 
-    arrived_mid = jnp.concatenate(arrived_parts, axis=1).astype(jnp.float32)
-    arrived = rms_scale(arrived_mid, moe_gain).astype(jnp.bfloat16)
-
     gate_up = w_gate_up[0]
     down_proj = w_down[0]
     hidden_width = down_proj.shape[0]
-    projected_up = jnp.dot(arrived, gate_up, preferred_element_type=jnp.float32)
+    arrived_wide = [p.astype(jnp.float32) for p in arrived_parts]
+    square_sum = sum(jnp.sum(p * p, axis=-1, keepdims=True) for p in arrived_wide)
+    scale = lax.rsqrt(square_sum / feat_width + EPS)
+    projected_up = sum(
+        jnp.dot(
+            (p * scale * moe_gain[lo:hi]).astype(jnp.bfloat16),
+            gate_up[lo:hi],
+            preferred_element_type=jnp.float32,
+        )
+        for p, (lo, hi) in zip(arrived_wide, bounds)
+    )
     activated = (
         jax.nn.silu(projected_up[:, :hidden_width]) * projected_up[:, hidden_width:]
     ).astype(jnp.bfloat16)

time: 403 us -> 410 us (1.017)
  waiting for transfers between devices: 142 us -> 151 us
  other arithmetic: 8.54 us -> 15.4 us
    all_to_all x3 -> x2, waiting for transfers between devices: 95.5 us -> 104 us  [local(): lax.all_to_all(outgoing.reshape(experts, capacity, hi - lo), 'tp', split_...]
    convert_element_type x0 -> x2, other arithmetic: none -> 5.45 us  [local(): (p * scale * moe_gain[lo:hi]).astype(jnp.bfloat16)]
    reduce_sum x0 -> x2, other arithmetic: none -> 5.11 us  [local(): jnp.sum(p * p, axis=-1, keepdims=True)]
    reduce_sum x2 -> x1, other arithmetic: 4.57 us -> 0.19 us  [rms_scale(): mean_square = jnp.mean(values * values, axis=-1, keepdims=True)]
    dot_general x1 -> x2, matrix products: 9.11 us -> 6.87 us  [local(): jnp.dot((p * scale * moe_gain[lo:hi]).astype(jnp.bfloat16), gate_up[lo:hi...]
    dot_general x8 -> x4, matrix products: 10.6 us -> 9.25 us  [product(): return jnp.dot(rows, weights, preferred_element_type=jnp.float32)]
    all_to_all x3 -> x2, starting transfers between devices: 27 us -> 26.1 us  [local(): lax.all_to_all(outgoing.reshape(experts, capacity, hi - lo), 'tp', split_...]
    ppermute x6 -> x3, waiting for transfers between devices: 35.3 us -> 34.6 us  [dp_reduce(): total = total + lax.ppermute(product((here + shift) % ring), 'dp', pairs)]
  transfers between devices with their start and end apart: 10 -> 6, of which waited for: 10 -> 5; matrix products, arithmetic and copies ran while one was open for 5% -> 4% of each run, Pallas kernels for 0% -> 0%
where the time goes in v3:
time: 410 us
  blocking collectives  175 us (43%)
  waiting for transfers between devices  151 us (37%)
  starting transfers between devices  33.7 us (8%)
  matrix products  31.4 us (8%)
  other arithmetic  15.4 us (4%)
    all_to_all x1, blocking collectives, local(): lax.all_to_all(served.reshape(experts, capacity, feat_width), 'tp', split...  147 us
    all_to_all x2, waiting for transfers between devices, local(): lax.all_to_all(outgoing.reshape(experts, capacity, hi - lo), 'tp', split_...  104 us
    ppermute x3, waiting for transfers between devices, dp_reduce(): total = total + lax.ppermute(product((here + shift) % ring), 'dp', pairs)  34.6 us
    all_to_all x1, blocking collectives, local(): lax.all_to_all(copies, 'dp', split_axis=0, concat_axis=0, tiled=True)  28.7 us
    all_to_all x2, starting transfers between devices, local(): lax.all_to_all(outgoing.reshape(experts, capacity, hi - lo), 'tp', split_...  26.1 us
    all_to_all x1, waiting for transfers between devices, local(): lax.all_to_all(partial.reshape(groups, tok_rows, first), 'dp', split_axis...  12.2 us
    dot_general x4, matrix products, product(): return jnp.dot(rows, weights, preferred_element_type=jnp.float32)  9.25 us
  transfers between devices with their start and end apart: 6, of which 5 were waited for; matrix products, arithmetic and copies ran while one was open for 4% of the time, Pallas kernels for 0%

profile of v3, /device:TPU:1, one launch (start us, length us, event | category | flops | bytes accessed | tf_op | source)
XLA Modules:
  0.0 409.6 jit_solution(17124991318045484633)
XLA Ops:
  0.6 0.0 copy-start
  0.6 0.0 slice-start
  0.7 2.8 fusion.34
  3.4 5.0 %all-to-all-start = ((f32[4,128,512]{2,1,0:T(8,128)}), f32[4,128,512]{2,1,0:T(8,128)S(1)}, u32[]{:S(2)}, u32[]{:S(2)}) async-start(f32[4,128,512]{2,1,0:T(8,128)} %fusion.34), calls=%async_computation | async-start | bytes 2097152 | tf_op jit(solution)/shard_map/all_to_all | solution.py:60
  8.4 0.1 eq.44
  8.6 0.1 convolution_convert_fusion.3
  8.7 1.0 fusion.31
  9.7 12.2 %all-to-all-done = f32[4,128,512]{2,1,0:T(8,128)S(1)} async-done(((f32[4,128,512]{2,1,0:T(8,128)}), f32[4,128,512]{2,1,0:T(8,128)S(1)}, u32[]{:S(2)}, u32[]{:S(2)}) %all-to-all-start) | async-done | bytes 1048608 | tf_op jit(solution)/shard_map/all_to_all | solution.py:60
  21.9 0.8 reduce_sum.81
  22.7 1.0 add_convert_fusion.1
  23.8 2.6 convolution_convert_fusion.2
  26.4 14.2 %all-to-all-start.1 = ((bf16[64,24,512]{2,1,0:T(8,128)(2,1)}), bf16[64,24,512]{2,1,0:T(8,128)(2,1)}, u32[]{:S(2)}, u32[]{:S(2)}) async-start(bf16[64,24,512]{2,1,0:T(8,128)(2,1)} %bitcast.74), calls=%async_computation.1 | async-start | bytes 3145728 | tf_op jit(solution)/shard_map/all_to_all | solution.py:75
  40.6 0.0 copy-start.2
  40.7 2.8 fusion.21
  43.5 2.7 fusion.23
  46.2 1.3 fusion.25
  47.4 0.3 collective-permute-start
  47.7 1.8 collective-permute-start.1
  49.5 0.6 collective-permute-start.2
  50.1 18.0 %collective-permute-done = f32[128,1536]{1,0:T(8,128)} collective-permute-done((f32[128,1536]{1,0:T(8,128)}, f32[128,1536]{1,0:T(8,128)}, u32[]{:S(2)}, u32[]{:S(2)}) %collective-permute-start) | collective-permute-done | bytes 786464 | tf_op jit(solution)/shard_map/ppermute | solution.py:32
  68.1 15.7 %collective-permute-done.1 = f32[128,1536]{1,0:T(8,128)} collective-permute-done((f32[128,1536]{1,0:T(8,128)}, f32[128,1536]{1,0:T(8,128)}, u32[]{:S(2)}, u32[]{:S(2)}) %collective-permute-start.1) | collective-permute-done | bytes 786464 | tf_op jit(solution)/shard_map/ppermute | solution.py:32
  83.8 0.9 collective-permute-done.2
  84.8 2.5 fusion.11
  87.3 0.1 add_convert_fusion
  87.4 3.5 convolution_convert_fusion.1
  90.9 11.9 %all-to-all-start.2 = ((bf16[64,24,1536]{2,1,0:T(8,128)(2,1)}), bf16[64,24,1536]{2,1,0:T(8,128)(2,1)}, u32[]{:S(2)}, u32[]{:S(2)}) async-start(bf16[64,24,1536]{2,1,0:T(8,128)(2,1)} %bitcast.71), calls=%async_computation.2 | async-start | bytes 9437184 | tf_op jit(solution)/shard_map/all_to_all | solution.py:75
  102.8 0.2 fusion.16
  103.0 0.4 fusion.32
  103.5 0.3 fusion.30
  103.8 0.3 fusion.29
  104.1 1.8 fusion.3
  105.9 104.0 %all-to-all-done.2 = bf16[64,24,1536]{2,1,0:T(8,128)(2,1)} async-done(((bf16[64,24,1536]{2,1,0:T(8,128)(2,1)}), bf16[64,24,1536]{2,1,0:T(8,128)(2,1)}, u32[]{:S(2)}, u32[]{:S(2)}) %all-to-all-start.2) | async-done | bytes 4718624 | tf_op jit(solution)/shard_map/all_to_all | solution.py:75
  209.9 3.3 fusion
  213.2 0.0 copy-start.5
  213.3 3.6 fusion.2
  216.9 0.0 slice-start.2
  216.9 5.1 %fusion.7 = f32[1536,1024]{1,0:T(8,128)S(1)} fusion(bf16[1536,1536]{1,0:T(8,128)(2,1)S(1)} %bitcast.75, bf16[1,2048,1024]{2,1,0:T(8,128)(2,1)S(1)} %copy-done.5), kind=kOutput, calls=%fused_computation.15 | convolution fusion | flops 4831838208 | bytes 14155776 | tf_op jit(solution)/shard_map/dot_general | solution.py:97
  222.0 1.8 fusion.5
  223.8 1.8 convolution_add_fusion
  225.7 3.7 convolution_convert_fusion
  229.3 146.7 %all_to_all.25 = bf16[64,24,2048]{2,1,0:T(8,128)(2,1)S(1)} all-to-all(bf16[64,24,2048]{2,1,0:T(8,128)(2,1)S(1)} %bitcast.73), channel_id=1, replica_groups=mesh['dp'=4,'tp'=64] {'tp'}, dimensions={0} | all-to-all | bytes 12582912 | tf_op jit(solution)/shard_map/all_to_all | solution.py:110
  376.1 1.0 fusion.54
  377.1 0.0 copy-start.8
  377.1 1.1 multiply_reduce_fusion
  378.3 1.0 multiply_convert_fusion
  379.3 0.2 broadcast_in_dim.44
  379.5 28.7 %all_to_all.26 = bf16[4,128,2048]{2,1,0:T(8,128)(2,1)S(1)} all-to-all(bf16[4,128,2048]{2,1,0:T(8,128)(2,1)S(1)} %broadcast_in_dim.44), channel_id=1, replica_groups=mesh['dp'=4,'tp'=64] {'dp'}, dimensions={0} | all-to-all | bytes 4194304 | tf_op jit(solution)/shard_map/all_to_all | solution.py:122
  408.3 1.3 copy.21
  (32 shorter events, 0.2 us)
Async XLA Ops:
  0.6 225.0 %copy-start = (bf16[1,512,2048]{2,1,0:T(8,128)(2,1)S(1)}, bf16[1,512,2048]{2,1,0:T(8,128)(2,1)}, u32[]{:S(2)}) copy-start(bf16[1,512,2048]{2,1,0:T(8,128)(2,1)} %param.16) | copy-start | bytes 6291460
  0.6 22.1 %slice-start = ((bf16[128,2048]{1,0:T(8,128)(2,1)}), bf16[128,512]{1,0:T(8,128)(2,1)S(1)}, s32[]{:S(2)}) async-start(bf16[128,2048]{1,0:T(8,128)(2,1)} %param.11), calls=%async_computation.5 | async-start | bytes 262144 | tf_op jit(solution)/shard_map/slice | solution.py:67
  0.7 7.9 %copy-start.6 = (s32[128,8]{0,1:T(8,128)S(1)}, s32[128,8]{0,1:T(8,128)}, u32[]{:S(2)}) copy-start(s32[128,8]{0,1:T(8,128)} %param.14) | copy-start | bytes 12292
  3.4 18.5 %all-to-all-start = ((f32[4,128,512]{2,1,0:T(8,128)}), f32[4,128,512]{2,1,0:T(8,128)S(1)}, u32[]{:S(2)}, u32[]{:S(2)}) async-start(f32[4,128,512]{2,1,0:T(8,128)} %fusion.34), calls=%async_computation | async-start | bytes 2097152 | tf_op jit(solution)/shard_map/all_to_all | solution.py:60
  22.7 17.9 %copy-start.3 = (bf16[4,128,512]{2,1,0:T(8,128)(2,1)S(1)}, bf16[4,128,512]{2,1,0:T(8,128)(2,1)}, u32[]{:S(2)}) copy-start(bf16[4,128,512]{2,1,0:T(8,128)(2,1)} %param.9) | copy-start | bytes 1572868
  26.4 64.5 %all-to-all-start.1 = ((bf16[64,24,512]{2,1,0:T(8,128)(2,1)}), bf16[64,24,512]{2,1,0:T(8,128)(2,1)}, u32[]{:S(2)}, u32[]{:S(2)}) async-start(bf16[64,24,512]{2,1,0:T(8,128)(2,1)} %bitcast.74), calls=%async_computation.1 | async-start | bytes 3145728 | tf_op jit(solution)/shard_map/all_to_all | solution.py:75
  40.6 5.5 %copy-start.2 = (bf16[512,2048]{1,0:T(8,128)(2,1)S(1)}, bf16[512,2048]{1,0:T(8,128)(2,1)}, u32[]{:S(2)}) copy-start(bf16[512,2048]{1,0:T(8,128)(2,1)} %param.10) | copy-start | bytes 6291460
  47.4 39.8 %slice-start.1 = ((bf16[128,2048]{1,0:T(8,128)(2,1)}), bf16[128,1536]{1,0:T(8,128)(2,1)S(1)}, s32[]{:S(2)}) async-start(bf16[128,2048]{1,0:T(8,128)(2,1)} %param.11), calls=%async_computation.6 | async-start | bytes 786432 | tf_op jit(solution)/shard_map/slice | solution.py:67
  47.4 20.7 %collective-permute-start = (f32[128,1536]{1,0:T(8,128)}, f32[128,1536]{1,0:T(8,128)}, u32[]{:S(2)}, u32[]{:S(2)}) collective-permute-start(f32[128,1536]{1,0:T(8,128)} %fusion.25), channel_id=1, source_target_pairs={{0,64},{64,128},{128,192},{192,0},{1,65},{65,129},{129,193},{193,1... | collective-permute-start | bytes 2359304 | tf_op jit(solution)/shard_map/ppermute | solution.py:32
  47.7 36.1 %collective-permute-start.1 = (f32[128,1536]{1,0:T(8,128)}, f32[128,1536]{1,0:T(8,128)}, u32[]{:S(2)}, u32[]{:S(2)}) collective-permute-start(f32[128,1536]{1,0:T(8,128)} %fusion.23), channel_id=1, source_target_pairs={{0,128},{64,192},{128,0},{192,64},{1,129},{65,193},{129,1},{193,65... | collective-permute-start | bytes 2359304 | tf_op jit(solution)/shard_map/ppermute | solution.py:32
  49.5 35.3 %collective-permute-start.2 = (f32[128,1536]{1,0:T(8,128)}, f32[128,1536]{1,0:T(8,128)}, u32[]{:S(2)}, u32[]{:S(2)}) collective-permute-start(f32[128,1536]{1,0:T(8,128)} %fusion.21), channel_id=1, source_target_pairs={{0,192},{64,0},{128,64},{192,128},{1,193},{65,1},{129,65},{193,129... | collective-permute-start | bytes 2359304 | tf_op jit(solution)/shard_map/ppermute | solution.py:32
  50.1 37.3 %copy-start.4 = (pred[1536,128]{1,0:T(32,128)(4,1)S(1)}, pred[1536,128]{1,0:T(32,128)(4,1)}, u32[]{:S(2)}) copy-start(pred[1536,128]{1,0:T(32,128)(4,1)} %fusion.31) | copy-start | bytes 589828
  90.9 11.9 %copy-start.7 = (f32[2048]{0:T(1024)S(1)}, f32[2048]{0:T(1024)}, u32[]{:S(2)}) copy-start(f32[2048]{0:T(1024)} %param.12) | copy-start | bytes 24580
  90.9 12.1 %copy-start.9 = (bf16[2048,64]{0,1:T(8,128)(2,1)S(1)}, bf16[2048,64]{0,1:T(8,128)(2,1)}, u32[]{:S(2)}) copy-start(bf16[2048,64]{0,1:T(8,128)(2,1)} %param.13) | copy-start | bytes 786436
  90.9 119.0 %all-to-all-start.2 = ((bf16[64,24,1536]{2,1,0:T(8,128)(2,1)}), bf16[64,24,1536]{2,1,0:T(8,128)(2,1)}, u32[]{:S(2)}, u32[]{:S(2)}) async-start(bf16[64,24,1536]{2,1,0:T(8,128)(2,1)} %bitcast.71), calls=%async_computation.2 | async-start | bytes 9437184 | tf_op jit(solution)/shard_map/all_to_all | solution.py:75
  213.2 3.6 copy-start.5
  216.9 5.1 %slice-start.2 = ((f32[2048]{0:T(1024)}), f32[512]{0:T(512)S(1)}, s32[]{:S(2)}) async-start(f32[2048]{0:T(1024)} %param.12), calls=%async_computation.7 | async-start | bytes 4096 | tf_op jit(solution)/shard_map/slice | solution.py:98
  377.1 1.2 copy-start.8
  379.5 30.1 %copy-start.1 = (bf16[1,512,2048]{2,1,0:T(8,128)(2,1)S(1)}, bf16[1,512,2048]{2,1,0:T(8,128)(2,1)}, u32[]{:S(2)}) copy-start(bf16[1,512,2048]{2,1,0:T(8,128)(2,1)} %param.16) | copy-start | bytes 6291460

commit v4 on v2

--- a/solution.py
+++ b/solution.py
@@ -53,8 +53,8 @@
     placed = (member.T[:, None, :] > 0) & (row_ranks.T[:, None, :] == slot_pos[None, :, None])
     dispatch = placed.reshape(slots, tok_rows).astype(jnp.bfloat16)
 
-    first = feat_width // 4
-    bounds = [(0, first), (first, 2 * first), (2 * first, feat_width)]
+    first = 5 * feat_width // 16
+    bounds = [(0, first), (first, feat_width)]
     flat_heads = attn_heads.reshape(groups * tok_rows, quarter)
     partial = jnp.dot(flat_heads, w_out[:, :first], preferred_element_type=jnp.float32)
     pieces = lax.all_to_all(
@@ -68,10 +68,9 @@
         mid_c = (res_c.astype(jnp.float32) + part).astype(jnp.bfloat16)
         mid_parts.append(mid_c)
         outgoing = jnp.dot(dispatch, mid_c, preferred_element_type=jnp.float32).astype(jnp.bfloat16)
-        if c + 1 < len(bounds):
+        if c == 0:
             outgoing, heads_now = lax.optimization_barrier((outgoing, attn_heads))
-            next_lo, next_hi = bounds[c + 1]
-            part = dp_reduce(heads_now, w_out[:, next_lo:next_hi])
+            part = dp_reduce(heads_now, w_out[:, first:])
         arrived_parts.append(
             lax.all_to_all(
                 outgoing.reshape(experts, capacity, hi - lo), "tp", split_axis=0, concat_axis=0, tiled=True

time: 403 us -> 399 us (0.990)
  starting transfers between devices: 37.5 us -> 32.6 us
    ppermute x6 -> x3, waiting for transfers between devices: 35.3 us -> 31.8 us  [dp_reduce(): total = total + lax.ppermute(product((here + shift) % ring), 'dp', pairs)]
    all_to_all x3 -> x2, waiting for transfers between devices: 95.5 us -> 98.6 us  [local(): lax.all_to_all(outgoing.reshape(experts, capacity, hi - lo), 'tp', split_...]
    all_to_all x3 -> x2, starting transfers between devices: 27 us -> 24.9 us  [local(): lax.all_to_all(outgoing.reshape(experts, capacity, hi - lo), 'tp', split_...]
    dot_general x8 -> x4, matrix products: 10.6 us -> 8.96 us  [product(): return jnp.dot(rows, weights, preferred_element_type=jnp.float32)]
  transfers between devices with their start and end apart: 10 -> 6, of which waited for: 10 -> 6; matrix products, arithmetic and copies ran while one was open for 5% -> 4% of each run, Pallas kernels for 0% -> 0%
where the time goes in v4:
time: 399 us
  blocking collectives  175 us (44%)
  waiting for transfers between devices  144 us (36%)
  matrix products  33.6 us (8%)
  starting transfers between devices  32.6 us (8%)
  other arithmetic  9.22 us (2%)
    all_to_all x1, blocking collectives, local(): lax.all_to_all(served.reshape(experts, capacity, feat_width), 'tp', split...  147 us
    all_to_all x2, waiting for transfers between devices, local(): lax.all_to_all(outgoing.reshape(experts, capacity, hi - lo), 'tp', split_...  98.6 us
    ppermute x3, waiting for transfers between devices, dp_reduce(): total = total + lax.ppermute(product((here + shift) % ring), 'dp', pairs)  31.8 us
    all_to_all x1, blocking collectives, local(): lax.all_to_all(copies, 'dp', split_axis=0, concat_axis=0, tiled=True)  28.6 us
    all_to_all x2, starting transfers between devices, local(): lax.all_to_all(outgoing.reshape(experts, capacity, hi - lo), 'tp', split_...  24.9 us
    all_to_all x1, waiting for transfers between devices, local(): lax.all_to_all(partial.reshape(groups, tok_rows, first), 'dp', split_axis...  13.5 us
    dot_general x1, matrix products, local(): projected_up = jnp.dot(arrived, gate_up, preferred_element_type=jnp.float32)  9.03 us
    dot_general x4, matrix products, product(): return jnp.dot(rows, weights, preferred_element_type=jnp.float32)  8.96 us
  transfers between devices with their start and end apart: 6, of which 6 were waited for; matrix products, arithmetic and copies ran while one was open for 4% of the time, Pallas kernels for 0%

profile of v4, /device:TPU:1, one launch (start us, length us, event | category | flops | bytes accessed | tf_op | source)
XLA Modules:
  0.0 398.7 jit_solution(7732363463201043012)
XLA Ops:
  0.6 0.0 copy-start
  0.7 3.0 fusion.29
  3.7 5.0 %all-to-all-start = ((f32[4,128,640]{2,1,0:T(8,128)}), f32[4,128,640]{2,1,0:T(8,128)S(1)}, u32[]{:S(2)}, u32[]{:S(2)}) async-start(f32[4,128,640]{2,1,0:T(8,128)} %fusion.29), calls=%async_computation | async-start | bytes 2621440 | tf_op jit(solution)/shard_map/all_to_all | solution.py:60
  8.7 0.1 eq.44
  8.8 1.6 slice.18
  10.4 0.0 copy-done.4
  10.4 0.1 convolution_convert_fusion.3
  10.6 1.0 fusion.28
  11.5 13.5 %all-to-all-done = f32[4,128,640]{2,1,0:T(8,128)S(1)} async-done(((f32[4,128,640]{2,1,0:T(8,128)}), f32[4,128,640]{2,1,0:T(8,128)S(1)}, u32[]{:S(2)}, u32[]{:S(2)}) %all-to-all-start) | async-done | bytes 1310752 | tf_op jit(solution)/shard_map/all_to_all | solution.py:60
  25.0 0.8 reduce_sum.72
  25.8 1.0 add_convert_fusion.1
  26.8 0.0 copy-start.2
  26.8 2.9 convolution_convert_fusion.2
  29.8 14.2 %all-to-all-start.1 = ((bf16[64,24,640]{2,1,0:T(8,128)(2,1)}), bf16[64,24,640]{2,1,0:T(8,128)(2,1)}, u32[]{:S(2)}, u32[]{:S(2)}) async-start(bf16[64,24,640]{2,1,0:T(8,128)(2,1)} %bitcast.67), calls=%async_computation.1 | async-start | bytes 3932160 | tf_op jit(solution)/shard_map/all_to_all | solution.py:75
  44.0 0.0 copy-start.1
  44.1 2.7 fusion.18
  46.8 2.6 fusion.20
  49.4 1.2 fusion.22
  50.7 0.3 collective-permute-start
  51.0 1.8 collective-permute-start.1
  52.7 0.6 collective-permute-start.2
  53.4 16.6 %collective-permute-done = f32[128,1408]{1,0:T(8,128)} collective-permute-done((f32[128,1408]{1,0:T(8,128)}, f32[128,1408]{1,0:T(8,128)}, u32[]{:S(2)}, u32[]{:S(2)}) %collective-permute-start) | collective-permute-done | bytes 720928 | tf_op jit(solution)/shard_map/ppermute | solution.py:32
  69.9 14.3 %collective-permute-done.1 = f32[128,1408]{1,0:T(8,128)} collective-permute-done((f32[128,1408]{1,0:T(8,128)}, f32[128,1408]{1,0:T(8,128)}, u32[]{:S(2)}, u32[]{:S(2)}) %collective-permute-start.1) | collective-permute-done | bytes 720928 | tf_op jit(solution)/shard_map/ppermute | solution.py:32
  84.3 0.9 collective-permute-done.2
  85.2 2.4 fusion.10
  87.6 0.0 slice-done
  87.6 0.1 add_convert_fusion
  87.6 3.3 convolution_convert_fusion.1
  90.9 1.2 all-to-all-done.1
  92.1 10.7 %all-to-all-start.2 = ((bf16[64,24,1408]{2,1,0:T(8,128)(2,1)}), bf16[64,24,1408]{2,1,0:T(8,128)(2,1)}, u32[]{:S(2)}, u32[]{:S(2)}) async-start(bf16[64,24,1408]{2,1,0:T(8,128)(2,1)} %bitcast.66), calls=%async_computation.2 | async-start | bytes 8650752 | tf_op jit(solution)/shard_map/all_to_all | solution.py:75
  102.8 0.2 fusion.15
  103.0 0.0 copy-done.7
  103.0 0.4 fusion.32
  103.5 0.3 fusion.27
  103.8 0.3 fusion.26
  104.1 97.4 %all-to-all-done.2 = bf16[64,24,1408]{2,1,0:T(8,128)(2,1)} async-done(((bf16[64,24,1408]{2,1,0:T(8,128)(2,1)}), bf16[64,24,1408]{2,1,0:T(8,128)(2,1)}, u32[]{:S(2)}, u32[]{:S(2)}) %all-to-all-start.2) | async-done | bytes 4325408 | tf_op jit(solution)/shard_map/all_to_all | solution.py:75
  201.5 4.4 %fusion = f32[1536]{0:T(1024)S(1)} fusion(bf16[1536,1408]{1,0:T(8,128)(2,1)} %bitcast.11, bf16[1536,640]{1,0:T(8,128)(2,1)} %bitcast.9), kind=kLoop, calls=%fused_computation.2 | loop fusion | flops 18872832 | bytes 6297600 | tf_op jit(solution)/shard_map/reduce_sum | solution.py:11
  205.9 0.0 copy-done.6
  205.9 9.0 %fusion.3 = f32[1536,1024]{1,0:T(8,128)S(1)} fusion(f32[2048]{0:T(1024)S(1)} %copy-done.8, f32[1536]{0:T(1024)S(1)} %add_rsqrt_fusion, bf16[1,2048,1024]{2,1,0:T(8,128)(2,1)S(1)} %copy-done.6, bf16[1536,1408]{1,0:T(8,128)(2,1)} %bitcast.11, bf16[1536,640]{1,0:T(8,128)(2,1)} %bitcast.9), kind=kOutput, calls=%fused_computation.7 | convolution fusion | flops 6464471040 | bytes 16791552 | tf_op jit(solution)/shard_map/dot_general | solution.py:96
  215.0 3.7 convolution_convert_fusion
  218.7 146.6 %all_to_all.25 = bf16[64,24,2048]{2,1,0:T(8,128)(2,1)S(1)} all-to-all(bf16[64,24,2048]{2,1,0:T(8,128)(2,1)S(1)} %bitcast.68), channel_id=1, replica_groups=mesh['dp'=4,'tp'=64] {'tp'}, dimensions={0} | all-to-all | bytes 12582912 | tf_op jit(solution)/shard_map/all_to_all | solution.py:103
  365.3 1.0 fusion.52
  366.3 0.0 copy-start.5
  366.3 1.1 multiply_reduce_fusion
  367.5 1.0 multiply_convert_fusion
  368.5 0.2 broadcast_in_dim.44
  368.8 28.6 %all_to_all.26 = bf16[4,128,2048]{2,1,0:T(8,128)(2,1)S(1)} all-to-all(bf16[4,128,2048]{2,1,0:T(8,128)(2,1)S(1)} %broadcast_in_dim.44), channel_id=1, replica_groups=mesh['dp'=4,'tp'=64] {'dp'}, dimensions={0} | all-to-all | bytes 4194304 | tf_op jit(solution)/shard_map/all_to_all | solution.py:115
  397.4 1.3 copy.21
  (22 shorter events, 0.2 us)
Async XLA Ops:
  0.6 214.3 %copy-start = (bf16[1,512,2048]{2,1,0:T(8,128)(2,1)S(1)}, bf16[1,512,2048]{2,1,0:T(8,128)(2,1)}, u32[]{:S(2)}) copy-start(bf16[1,512,2048]{2,1,0:T(8,128)(2,1)} %param.16) | copy-start | bytes 6291460
  0.6 9.7 %copy-start.4 = (s32[128,8]{0,1:T(8,128)S(1)}, s32[128,8]{0,1:T(8,128)}, u32[]{:S(2)}) copy-start(s32[128,8]{0,1:T(8,128)} %param.14) | copy-start | bytes 12292
  3.7 21.3 %all-to-all-start = ((f32[4,128,640]{2,1,0:T(8,128)}), f32[4,128,640]{2,1,0:T(8,128)S(1)}, u32[]{:S(2)}, u32[]{:S(2)}) async-start(f32[4,128,640]{2,1,0:T(8,128)} %fusion.29), calls=%async_computation | async-start | bytes 2621440 | tf_op jit(solution)/shard_map/all_to_all | solution.py:60
  26.8 17.2 %copy-start.2 = (bf16[4,128,512]{2,1,0:T(8,128)(2,1)S(1)}, bf16[4,128,512]{2,1,0:T(8,128)(2,1)}, u32[]{:S(2)}) copy-start(bf16[4,128,512]{2,1,0:T(8,128)(2,1)} %param.9) | copy-start | bytes 1572868
  29.8 62.3 %all-to-all-start.1 = ((bf16[64,24,640]{2,1,0:T(8,128)(2,1)}), bf16[64,24,640]{2,1,0:T(8,128)(2,1)}, u32[]{:S(2)}, u32[]{:S(2)}) async-start(bf16[64,24,640]{2,1,0:T(8,128)(2,1)} %bitcast.67), calls=%async_computation.1 | async-start | bytes 3932160 | tf_op jit(solution)/shard_map/all_to_all | solution.py:75
  44.0 5.4 %copy-start.1 = (bf16[512,2048]{1,0:T(8,128)(2,1)S(1)}, bf16[512,2048]{1,0:T(8,128)(2,1)}, u32[]{:S(2)}) copy-start(bf16[512,2048]{1,0:T(8,128)(2,1)} %param.10) | copy-start | bytes 6291460
  50.7 36.9 %slice-start = ((bf16[128,2048]{1,0:T(8,128)(2,1)}), bf16[128,1408]{1,0:T(8,128)(2,1)S(1)}, s32[]{:S(2)}) async-start(bf16[128,2048]{1,0:T(8,128)(2,1)} %param.11), calls=%async_computation.5 | async-start | bytes 720896 | tf_op jit(solution)/shard_map/slice | solution.py:67
  50.7 19.3 %collective-permute-start = (f32[128,1408]{1,0:T(8,128)}, f32[128,1408]{1,0:T(8,128)}, u32[]{:S(2)}, u32[]{:S(2)}) collective-permute-start(f32[128,1408]{1,0:T(8,128)} %fusion.22), channel_id=1, source_target_pairs={{0,64},{64,128},{128,192},{192,0},{1,65},{65,129},{129,193},{193,1... | collective-permute-start | bytes 2162696 | tf_op jit(solution)/shard_map/ppermute | solution.py:32
  51.0 33.3 %collective-permute-start.1 = (f32[128,1408]{1,0:T(8,128)}, f32[128,1408]{1,0:T(8,128)}, u32[]{:S(2)}, u32[]{:S(2)}) collective-permute-start(f32[128,1408]{1,0:T(8,128)} %fusion.20), channel_id=1, source_target_pairs={{0,128},{64,192},{128,0},{192,64},{1,129},{65,193},{129,1},{193,65... | collective-permute-start | bytes 2162696 | tf_op jit(solution)/shard_map/ppermute | solution.py:32
  52.7 32.4 %collective-permute-start.2 = (f32[128,1408]{1,0:T(8,128)}, f32[128,1408]{1,0:T(8,128)}, u32[]{:S(2)}, u32[]{:S(2)}) collective-permute-start(f32[128,1408]{1,0:T(8,128)} %fusion.18), channel_id=1, source_target_pairs={{0,192},{64,0},{128,64},{192,128},{1,193},{65,1},{129,65},{193,129... | collective-permute-start | bytes 2162696 | tf_op jit(solution)/shard_map/ppermute | solution.py:32
  53.4 34.3 %copy-start.3 = (pred[1536,128]{1,0:T(32,128)(4,1)S(1)}, pred[1536,128]{1,0:T(32,128)(4,1)}, u32[]{:S(2)}) copy-start(pred[1536,128]{1,0:T(32,128)(4,1)} %fusion.28) | copy-start | bytes 589828
  92.1 10.9 %copy-start.7 = (bf16[2048,64]{0,1:T(8,128)(2,1)S(1)}, bf16[2048,64]{0,1:T(8,128)(2,1)}, u32[]{:S(2)}) copy-start(bf16[2048,64]{0,1:T(8,128)(2,1)} %param.13) | copy-start | bytes 786436
  92.1 10.9 %copy-start.8 = (f32[2048]{0:T(1024)S(1)}, f32[2048]{0:T(1024)}, u32[]{:S(2)}) copy-start(f32[2048]{0:T(1024)} %param.12) | copy-start | bytes 24580
  92.1 109.4 %all-to-all-start.2 = ((bf16[64,24,1408]{2,1,0:T(8,128)(2,1)}), bf16[64,24,1408]{2,1,0:T(8,128)(2,1)}, u32[]{:S(2)}, u32[]{:S(2)}) async-start(bf16[64,24,1408]{2,1,0:T(8,128)(2,1)} %bitcast.66), calls=%async_computation.2 | async-start | bytes 8650752 | tf_op jit(solution)/shard_map/all_to_all | solution.py:75
  201.5 4.4 %copy-start.6 = (bf16[1,2048,1024]{2,1,0:T(8,128)(2,1)S(1)}, bf16[1,2048,1024]{2,1,0:T(8,128)(2,1)}, u32[]{:S(2)}) copy-start(bf16[1,2048,1024]{2,1,0:T(8,128)(2,1)} %param.15) | copy-start | bytes 12582916
  366.3 1.2 copy-start.5

commit v5 on v4

--- a/solution.py
+++ b/solution.py
@@ -34,7 +34,7 @@
 
 
 def local(attn_heads, w_out, residual, moe_gain, router, expert_ids, w_gate_up, w_down, next_gain):
-    groups, tok_rows, quarter = attn_heads.shape
+    groups, tok_rows, _ = attn_heads.shape
     feat_width = w_out.shape[1]
     experts = router.shape[1]
     top_count = expert_ids.shape[1]
@@ -53,14 +53,9 @@
     placed = (member.T[:, None, :] > 0) & (row_ranks.T[:, None, :] == slot_pos[None, :, None])
     dispatch = placed.reshape(slots, tok_rows).astype(jnp.bfloat16)
 
-    first = 5 * feat_width // 16
+    first = feat_width // 4
     bounds = [(0, first), (first, feat_width)]
-    flat_heads = attn_heads.reshape(groups * tok_rows, quarter)
-    partial = jnp.dot(flat_heads, w_out[:, :first], preferred_element_type=jnp.float32)
-    pieces = lax.all_to_all(
-        partial.reshape(groups, tok_rows, first), "dp", split_axis=0, concat_axis=0, tiled=True
-    )
-    part = jnp.sum(pieces, axis=0)
+    part = dp_reduce(attn_heads, w_out[:, :first])
     mid_parts = []
     arrived_parts = []
     for c, (lo, hi) in enumerate(bounds):

time: 399 us -> 401 us (level)
    all_to_all x1 -> x0, waiting for transfers between devices: 13.5 us -> none  [local(): lax.all_to_all(partial.reshape(groups, tok_rows, first), 'dp', split_axis...]
    ppermute x3 -> x6, waiting for transfers between devices: 31.8 us -> 42.4 us  [dp_reduce(): total = total + lax.ppermute(product((here + shift) % ring), 'dp', pairs)]
    all_to_all x2, waiting for transfers between devices: 98.6 us -> 106 us  [local(): lax.all_to_all(outgoing.reshape(experts, capacity, hi - lo), 'tp', split_...]
    ppermute x3 -> x6, starting transfers between devices: 2.69 us -> 7.95 us  [dp_reduce(): total = total + lax.ppermute(product((here + shift) % ring), 'dp', pairs)]
    all_to_all x1 -> x0, starting transfers between devices: 5 us -> none  [local(): lax.all_to_all(partial.reshape(groups, tok_rows, first), 'dp', split_axis...]
    dot_general x4 -> x8, matrix products: 8.96 us -> 12.4 us  [product(): return jnp.dot(rows, weights, preferred_element_type=jnp.float32)]
  transfers between devices with their start and end apart: 6 -> 8, of which waited for: 6 -> 5; matrix products, arithmetic and copies ran while one was open for 4% -> 4% of each run, Pallas kernels for 0% -> 0%
where the time goes in v5:
time: 401 us
  blocking collectives  175 us (44%)
  waiting for transfers between devices  148 us (37%)
  starting transfers between devices  34.3 us (9%)
  matrix products  33 us (8%)
  other arithmetic  7.43 us (2%)
    all_to_all x1, blocking collectives, local(): lax.all_to_all(served.reshape(experts, capacity, feat_width), 'tp', split...  147 us
    all_to_all x2, waiting for transfers between devices, local(): lax.all_to_all(outgoing.reshape(experts, capacity, hi - lo), 'tp', split_...  106 us
    ppermute x6, waiting for transfers between devices, dp_reduce(): total = total + lax.ppermute(product((here + shift) % ring), 'dp', pairs)  42.4 us
    all_to_all x1, blocking collectives, local(): lax.all_to_all(copies, 'dp', split_axis=0, concat_axis=0, tiled=True)  28.6 us
    all_to_all x2, starting transfers between devices, local(): lax.all_to_all(outgoing.reshape(experts, capacity, hi - lo), 'tp', split_...  26.3 us
    dot_general x8, matrix products, product(): return jnp.dot(rows, weights, preferred_element_type=jnp.float32)  12.4 us
    dot_general x1, matrix products, local(): projected_up = jnp.dot(arrived, gate_up, preferred_element_type=jnp.float32)  9.01 us
  transfers between devices with their start and end apart: 8, of which 5 were waited for; matrix products, arithmetic and copies ran while one was open for 4% of the time, Pallas kernels for 0%

profile of v5, /device:TPU:1, one launch (start us, length us, event | category | flops | bytes accessed | tf_op | source)
XLA Modules:
  0.0 400.9 jit_solution(3427482890844551236)
XLA Ops:
  0.6 0.0 copy-start
  0.6 0.0 copy-start.2
  0.7 0.0 slice-start
  0.7 2.2 fusion.35
  2.9 3.6 collective-permute-start.2
  6.5 2.0 fusion.39
  8.5 2.0 fusion.37
  10.6 1.6 collective-permute-start.1
  12.2 0.7 convert_reduce_fusion
  13.0 0.1 eq.47
  13.0 0.1 convolution_convert_fusion.3
  13.2 0.3 fusion.30
  13.5 0.0 copy-start.3
  13.5 4.5 %collective-permute-done = f32[128,512]{1,0:T(8,128)} collective-permute-done((f32[128,512]{1,0:T(8,128)}, f32[128,512]{1,0:T(8,128)}, u32[]{:S(2)}, u32[]{:S(2)}) %collective-permute-start) | collective-permute-done | bytes 262176 | tf_op jit(solution)/shard_map/ppermute | solution.py:32
  18.0 3.6 collective-permute-done.1
  21.6 1.5 fusion.16
  23.1 1.7 convolution_convert_fusion.2
  24.8 14.5 %all-to-all-start = ((bf16[64,24,512]{2,1,0:T(8,128)(2,1)}), bf16[64,24,512]{2,1,0:T(8,128)(2,1)}, u32[]{:S(2)}, u32[]{:S(2)}) async-start(bf16[64,24,512]{2,1,0:T(8,128)(2,1)} %bitcast.76), calls=%async_computation | async-start | bytes 3145728 | tf_op jit(solution)/shard_map/all_to_all | solution.py:70
  39.3 0.0 copy-start.1
  39.3 1.9 fusion.20
  41.3 1.8 fusion.22
  43.1 0.4 fusion.24
  43.5 0.0 slice-start.1
  43.5 0.1 collective-permute-start.3
  43.6 0.6 collective-permute-start.4
  44.1 2.1 collective-permute-start.5
  46.2 34.0 %collective-permute-done.3 = f32[128,1536]{1,0:T(8,128)S(1)} collective-permute-done((f32[128,1536]{1,0:T(8,128)S(1)}, f32[128,1536]{1,0:T(8,128)S(1)}, u32[]{:S(2)}, u32[]{:S(2)}) %collective-permute-start.3) | collective-permute-done | bytes 786464 | tf_op jit(solution)/shard_map/ppermute | solution.py:32
  80.2 0.4 collective-permute-done.5
  80.6 0.4 fusion.10
  81.0 0.1 add_convert_fusion
  81.1 3.5 convolution_convert_fusion.1
  84.7 11.9 %all-to-all-start.1 = ((bf16[64,24,1536]{2,1,0:T(8,128)(2,1)}), bf16[64,24,1536]{2,1,0:T(8,128)(2,1)}, u32[]{:S(2)}, u32[]{:S(2)}) async-start(bf16[64,24,1536]{2,1,0:T(8,128)(2,1)} %bitcast.74), calls=%async_computation.1 | async-start | bytes 9437184 | tf_op jit(solution)/shard_map/all_to_all | solution.py:70
  96.6 0.2 fusion.17
  96.8 0.4 fusion.31
  97.3 0.3 fusion.29
  97.6 0.3 fusion.28
  97.8 105.8 %all-to-all-done.1 = bf16[64,24,1536]{2,1,0:T(8,128)(2,1)} async-done(((bf16[64,24,1536]{2,1,0:T(8,128)(2,1)}), bf16[64,24,1536]{2,1,0:T(8,128)(2,1)}, u32[]{:S(2)}, u32[]{:S(2)}) %all-to-all-start.1) | async-done | bytes 4718624 | tf_op jit(solution)/shard_map/all_to_all | solution.py:70
  203.7 4.4 %fusion = f32[1536]{0:T(1024)S(1)} fusion(bf16[1536,1536]{1,0:T(8,128)(2,1)} %bitcast.14, bf16[1536,512]{1,0:T(8,128)(2,1)} %bitcast.12), kind=kLoop, calls=%fused_computation.2 | loop fusion | flops 18872832 | bytes 6297600 | tf_op jit(solution)/shard_map/reduce_sum | solution.py:11
  208.1 9.0 %fusion.3 = f32[1536,1024]{1,0:T(8,128)S(1)} fusion(f32[2048]{0:T(1024)S(1)} %copy-done.8, f32[1536]{0:T(1024)S(1)} %add_rsqrt_fusion, bf16[1,2048,1024]{2,1,0:T(8,128)(2,1)S(1)} %copy-done.6, bf16[1536,1536]{1,0:T(8,128)(2,1)} %bitcast.14, bf16[1536,512]{1,0:T(8,128)(2,1)} %bitcast.12), kind=kOutput, calls=%fused_computation.7 | convolution fusion | flops 6464471040 | bytes 16791552 | tf_op jit(solution)/shard_map/dot_general | solution.py:91
  217.1 3.7 convolution_convert_fusion
  220.8 146.7 %all_to_all.20 = bf16[64,24,2048]{2,1,0:T(8,128)(2,1)S(1)} all-to-all(bf16[64,24,2048]{2,1,0:T(8,128)(2,1)S(1)} %bitcast.75), channel_id=1, replica_groups=mesh['dp'=4,'tp'=64] {'tp'}, dimensions={0} | all-to-all | bytes 12582912 | tf_op jit(solution)/shard_map/all_to_all | solution.py:98
  367.5 1.0 fusion.70
  368.6 0.0 copy-start.5
  368.6 1.1 multiply_reduce_fusion
  369.7 1.0 multiply_convert_fusion
  370.8 0.2 broadcast_in_dim.44
  371.0 28.6 %all_to_all.21 = bf16[4,128,2048]{2,1,0:T(8,128)(2,1)S(1)} all-to-all(bf16[4,128,2048]{2,1,0:T(8,128)(2,1)S(1)} %broadcast_in_dim.44), channel_id=1, replica_groups=mesh['dp'=4,'tp'=64] {'dp'}, dimensions={0} | all-to-all | bytes 4194304 | tf_op jit(solution)/shard_map/all_to_all | solution.py:110
  399.6 1.3 copy.21
  (29 shorter events, 0.2 us)
Async XLA Ops:
  0.6 216.5 %copy-start = (bf16[1,512,2048]{2,1,0:T(8,128)(2,1)S(1)}, bf16[1,512,2048]{2,1,0:T(8,128)(2,1)}, u32[]{:S(2)}) copy-start(bf16[1,512,2048]{2,1,0:T(8,128)(2,1)} %param.16) | copy-start | bytes 6291460
  0.6 20.9 %copy-start.2 = (bf16[4,128,512]{2,1,0:T(8,128)(2,1)S(1)}, bf16[4,128,512]{2,1,0:T(8,128)(2,1)}, u32[]{:S(2)}) copy-start(bf16[4,128,512]{2,1,0:T(8,128)(2,1)} %param.9) | copy-start | bytes 1572868
  0.7 22.4 %slice-start = ((bf16[128,2048]{1,0:T(8,128)(2,1)}), bf16[128,512]{1,0:T(8,128)(2,1)S(1)}, s32[]{:S(2)}) async-start(bf16[128,2048]{1,0:T(8,128)(2,1)} %param.11), calls=%async_computation.4 | async-start | bytes 262144 | tf_op jit(solution)/shard_map/slice | solution.py:62
  2.9 10.6 %collective-permute-start.2 = (f32[128,512]{1,0:T(8,128)}, f32[128,512]{1,0:T(8,128)S(1)}, u32[]{:S(2)}, u32[]{:S(2)}) collective-permute-start(f32[128,512]{1,0:T(8,128)} %fusion.35), channel_id=1, source_target_pairs={{0,192},{64,0},{128,64},{192,128},{1,193},{65,1},{129,65},{193,129... | collective-permute-start | bytes 786440 | tf_op jit(solution)/shard_map/ppermute | solution.py:32
  8.5 9.5 %collective-permute-start = (f32[128,512]{1,0:T(8,128)}, f32[128,512]{1,0:T(8,128)}, u32[]{:S(2)}, u32[]{:S(2)}) collective-permute-start(f32[128,512]{1,0:T(8,128)} %fusion.39), channel_id=1, source_target_pairs={{0,64},{64,128},{128,192},{192,0},{1,65},{65,129},{129,193},{193,1... | collective-permute-start | bytes 786440 | tf_op jit(solution)/shard_map/ppermute | solution.py:32
  10.6 11.0 %collective-permute-start.1 = (f32[128,512]{1,0:T(8,128)}, f32[128,512]{1,0:T(8,128)}, u32[]{:S(2)}, u32[]{:S(2)}) collective-permute-start(f32[128,512]{1,0:T(8,128)} %fusion.37), channel_id=1, source_target_pairs={{0,128},{64,192},{128,0},{192,64},{1,129},{65,193},{129,1},{193,65... | collective-permute-start | bytes 786440 | tf_op jit(solution)/shard_map/ppermute | solution.py:32
  13.5 4.5 %copy-start.3 = (f32[128,512]{1,0:T(8,128)}, f32[128,512]{1,0:T(8,128)S(1)}, u32[]{:S(2)}) copy-start(f32[128,512]{1,0:T(8,128)S(1)} %collective-permute-done.2) | copy-start | bytes 786436
  24.8 59.8 %all-to-all-start = ((bf16[64,24,512]{2,1,0:T(8,128)(2,1)}), bf16[64,24,512]{2,1,0:T(8,128)(2,1)}, u32[]{:S(2)}, u32[]{:S(2)}) async-start(bf16[64,24,512]{2,1,0:T(8,128)(2,1)} %bitcast.76), calls=%async_computation | async-start | bytes 3145728 | tf_op jit(solution)/shard_map/all_to_all | solution.py:70
  39.3 3.7 copy-start.1
  43.5 37.5 %slice-start.1 = ((bf16[128,2048]{1,0:T(8,128)(2,1)}), bf16[128,1536]{1,0:T(8,128)(2,1)S(1)}, s32[]{:S(2)}) async-start(bf16[128,2048]{1,0:T(8,128)(2,1)} %param.11), calls=%async_computation.5 | async-start | bytes 786432 | tf_op jit(solution)/shard_map/slice | solution.py:62
  43.5 36.7 %collective-permute-start.3 = (f32[128,1536]{1,0:T(8,128)S(1)}, f32[128,1536]{1,0:T(8,128)S(1)}, u32[]{:S(2)}, u32[]{:S(2)}) collective-permute-start(f32[128,1536]{1,0:T(8,128)S(1)} %fusion.24), channel_id=1, source_target_pairs={{0,64},{64,128},{128,192},{192,0},{1,65},{65,129},{129,193},{193,1... | collective-permute-start | bytes 2359304 | tf_op jit(solution)/shard_map/ppermute | solution.py:32
  43.6 36.6 %collective-permute-start.4 = (f32[128,1536]{1,0:T(8,128)S(1)}, f32[128,1536]{1,0:T(8,128)S(1)}, u32[]{:S(2)}, u32[]{:S(2)}) collective-permute-start(f32[128,1536]{1,0:T(8,128)S(1)} %fusion.22), channel_id=1, source_target_pairs={{0,128},{64,192},{128,0},{192,64},{1,129},{65,193},{129,1},{193,65... | collective-permute-start | bytes 2359304 | tf_op jit(solution)/shard_map/ppermute | solution.py:32
  44.1 36.4 %collective-permute-start.5 = (f32[128,1536]{1,0:T(8,128)S(1)}, f32[128,1536]{1,0:T(8,128)S(1)}, u32[]{:S(2)}, u32[]{:S(2)}) collective-permute-start(f32[128,1536]{1,0:T(8,128)S(1)} %fusion.20), channel_id=1, source_target_pairs={{0,192},{64,0},{128,64},{192,128},{1,193},{65,1},{129,65},{193,129... | collective-permute-start | bytes 2359304 | tf_op jit(solution)/shard_map/ppermute | solution.py:32
  84.7 12.1 %copy-start.7 = (bf16[2048,64]{0,1:T(8,128)(2,1)S(1)}, bf16[2048,64]{0,1:T(8,128)(2,1)}, u32[]{:S(2)}) copy-start(bf16[2048,64]{0,1:T(8,128)(2,1)} %param.13) | copy-start | bytes 786436
  84.7 12.1 %copy-start.8 = (f32[2048]{0:T(1024)S(1)}, f32[2048]{0:T(1024)}, u32[]{:S(2)}) copy-start(f32[2048]{0:T(1024)} %param.12) | copy-start | bytes 24580
  84.7 12.5 %copy-start.4 = (s32[128,8]{0,1:T(8,128)S(1)}, s32[128,8]{0,1:T(8,128)}, u32[]{:S(2)}) copy-start(s32[128,8]{0,1:T(8,128)} %param.14) | copy-start | bytes 12292
  84.7 119.0 %all-to-all-start.1 = ((bf16[64,24,1536]{2,1,0:T(8,128)(2,1)}), bf16[64,24,1536]{2,1,0:T(8,128)(2,1)}, u32[]{:S(2)}, u32[]{:S(2)}) async-start(bf16[64,24,1536]{2,1,0:T(8,128)(2,1)} %bitcast.74), calls=%async_computation.1 | async-start | bytes 9437184 | tf_op jit(solution)/shard_map/all_to_all | solution.py:70
  203.7 4.4 %copy-start.6 = (bf16[1,2048,1024]{2,1,0:T(8,128)(2,1)S(1)}, bf16[1,2048,1024]{2,1,0:T(8,128)(2,1)}, u32[]{:S(2)}) copy-start(bf16[1,2048,1024]{2,1,0:T(8,128)(2,1)} %param.15) | copy-start | bytes 12582916
  368.6 1.2 copy-start.5
